TPU v7x, 128 devices: a whole 4x4x4 slice. The times are simulated.
128 devices in a mesh: section: 16 (over x, z_hi, core), expert: 8 (over z_lo, y).
Axes of the slice: x: 4, y: 4, z: 4 (z_hi: 2, z_lo: 2; z = z_hi * 2 + z_lo), core: 2. Of those that a mesh axis runs over, the one named last changes fastest.
Arguments:
- grad_in: bfloat16 [16, 1024, 4096], P('section', 'expert'), may hold values from -6 to 6
- saved_inputs: bfloat16 [3, 16, 1024, 4096], P(None, 'section', 'expert'), may hold values from -6 to 6
- expert_ids: int32 [3, 16, 1024, 2], P(None, 'section', 'expert'), may hold values from 0 to 7, as said below
- slots: int32 [3, 16, 1024, 2], P(None, 'section', 'expert'), may hold values from 0 to 36, as said below
- gates: float32 [3, 16, 1024, 2], P(None, 'section', 'expert'), may hold values from 0.05 to 0.8
- w_gate: bfloat16 [16, 8, 4096, 768], P('section', 'expert'), may hold values from -0.09375 to 0.09375
- w_up: bfloat16 [16, 8, 4096, 768], P('section', 'expert'), may hold values from -0.09375 to 0.09375
- w_down: bfloat16 [16, 8, 768, 4096], P('section', 'expert'), may hold values from -0.21875 to 0.21875
Outputs:
- grad_out: bfloat16 [16, 1024, 4096], P('section', 'expert')
Inputs may be any that keep to these rules, and one draw needn't show every extreme that they name: `expert_ids`: each token names 2 different experts; every expert is named. `slots`: among the routes of the tokens of one device (aligned blocks of 128 tokens) to one expert, taken in some order, the n-th has slot min(n, 36) for n = 0, 1, ...; in every round and section some such group has more than 36 routes.
All inputs are finite; a program needn't handle non-finite values.
Results may differ from a plain program's by a relative error of at most 0.0075.
Values may be sent and summed in bfloat16 or wider, within the bound.
No kernel may reach another device: no remote copies, remote signals or barrier semaphores. Data moves between devices by JAX's collectives and lax.ppermute only.
A program may use at most 128 MiB of HBM per device.

v0:
```python
import jax
import jax.numpy as jnp
from jax import lax
from jax.sharding import PartitionSpec as P


def shifted(x, axis, by):
    devices = lax.axis_size(axis)
    return lax.ppermute(x, axis, [(i, (i + by) % devices) for i in range(devices)])


def expert_pass(grad_part, input_part, gate_proj, up_proj, down_proj):
    pre_gate = jnp.dot(input_part, gate_proj, preferred_element_type=jnp.float32)
    pre_up = jnp.dot(input_part, up_proj, preferred_element_type=jnp.float32)
    grad_hidden = jnp.dot(grad_part, down_proj.T, preferred_element_type=jnp.float32)
    sigma = jax.nn.sigmoid(pre_gate)
    derivative = sigma * (1.0 + pre_gate * (1.0 - sigma))
    grad_gate = (grad_hidden * pre_up * derivative).astype(jnp.bfloat16)
    grad_up = (grad_hidden * pre_gate * sigma).astype(jnp.bfloat16)
    summed = jnp.dot(grad_gate, gate_proj.T, preferred_element_type=jnp.float32)
    summed = summed + jnp.dot(grad_up, up_proj.T, preferred_element_type=jnp.float32)
    return summed.astype(jnp.bfloat16)


def per_device(grad_in, saved_inputs, expert_ids, slots, gates, w_gate, w_up, w_down):
    groups = lax.axis_size("expert")
    rows_dev = grad_in.shape[1]
    width = grad_in.shape[2]
    rounds = saved_inputs.shape[0]
    capacity = 9 * rows_dev * expert_ids.shape[-1] // (8 * groups)
    gate_proj = w_gate[0, 0]
    up_proj = w_up[0, 0]
    down_proj = w_down[0, 0]
    token_ids = jnp.arange(rows_dev, dtype=jnp.int32)

    def route_plan(step):
        route_ids = expert_ids[step, 0]
        slot_ids = slots[step, 0]
        positions = jnp.where(
            slot_ids < capacity, route_ids * capacity + slot_ids, groups * capacity
        )
        owners = jnp.broadcast_to(token_ids[:, None], positions.shape).reshape(-1)
        sources = (
            jnp.full((groups * capacity,), rows_dev, jnp.int32)
            .at[positions.reshape(-1)]
            .set(owners, mode="drop")
        )
        return (positions, sources)

    def collect(rows, sources):
        return jnp.take(rows, sources, axis=0, mode="fill", fill_value=0).reshape(
            groups, capacity, width
        )

    plans = [route_plan(step) for step in range(rounds)]
    present_block = grad_in[0]
    for step in range(rounds):
        positions, sources = plans[step]
        grad_buffer = collect(present_block, sources)
        input_buffer = collect(saved_inputs[step, 0], sources)
        grad_part = lax.all_to_all(grad_buffer, "expert", split_axis=0, concat_axis=0, tiled=True)
        input_part = lax.all_to_all(input_buffer, "expert", split_axis=0, concat_axis=0, tiled=True)
        senders, count_rows, _ = grad_part.shape
        result = expert_pass(
            grad_part.reshape(senders * count_rows, width),
            input_part.reshape(senders * count_rows, width),
            gate_proj,
            up_proj,
            down_proj,
        )
        returned = result.reshape(senders, count_rows, width)
        arrived = lax.all_to_all(returned, "expert", split_axis=0, concat_axis=0, tiled=True)
        picked = jnp.take(
            arrived.reshape(groups * capacity, width), positions, axis=0, mode="fill", fill_value=0
        )
        summed = present_block.astype(jnp.float32) + jnp.sum(
            gates[step, 0][..., None] * picked.astype(jnp.float32), axis=1
        )
        present_block = shifted(summed.astype(jnp.bfloat16), "section", -1)
    return present_block[None]


def solution(mesh):
    placed = (
        P("section", "expert", None),
        P(None, "section", "expert", None),
        P(None, "section", "expert", None),
        P(None, "section", "expert", None),
        P(None, "section", "expert", None),
        P("section", "expert", None, None),
        P("section", "expert", None, None),
        P("section", "expert", None, None),
    )
    return jax.shard_map(
        per_device,
        mesh=mesh,
        in_specs=placed,
        out_specs=P("section", "expert", None),
        check_vma=False,
    )
```

profile of v0, /device:TPU:1, one launch (start us, length us, event | category | flops | bytes accessed | tf_op | source)
XLA Modules:
  0.0 658.4 jit_solution(9696236447884267631)
XLA Ops:
  6.3 9.4 %gather_fusion.1 = bf16[288,4096]{1,0:T(8,128)(2,1)} fusion(bf16[128,4096]{1,0:T(8,128)(2,1)} %get-tuple-element.14, s32[1024]{0:T(1024)S(1)} %pad_clamp_fusion.5), kind=kCustom, calls=%fused_computation.2.clone | custom fusion | bytes 4719744 | tf_op jit(solution)/shard_map/jit(_take)/gather | solution.py:51
  39.1 28.6 %all-to-all-done.1 = bf16[8,36,4096]{2,1,0:T(8,128)(2,1)} async-done(((bf16[8,36,4096]{2,1,0:T(8,128)(2,1)}), bf16[8,36,4096]{2,1,0:T(8,128)(2,1)}, u32[]{:S(2)}, u32[]{:S(2)}) %all-to-all-start.1) | async-done | bytes 2359328 | tf_op jit(solution)/shard_map/all_to_all | solution.py:62
  67.8 7.8 %all-to-all-start = ((bf16[8,36,4096]{2,1,0:T(8,128)(2,1)}), bf16[8,36,4096]{2,1,0:T(8,128)(2,1)}, u32[]{:S(2)}, u32[]{:S(2)}) async-start(bf16[8,36,4096]{2,1,0:T(8,128)(2,1)} %reshape.251), calls=%async_computation | async-start | bytes 5242880 | tf_op jit(solution)/shard_map/all_to_all | solution.py:61
  79.7 6.4 fusion.10
  86.1 22.2 %all-to-all-done = bf16[8,36,4096]{2,1,0:T(8,128)(2,1)} async-done(((bf16[8,36,4096]{2,1,0:T(8,128)(2,1)}), bf16[8,36,4096]{2,1,0:T(8,128)(2,1)}, u32[]{:S(2)}, u32[]{:S(2)}) %all-to-all-start) | async-done | bytes 2359328 | tf_op jit(solution)/shard_map/all_to_all | solution.py:61
  112.4 6.4 fusion.28
  118.9 13.0 %fusion.8 = f32[288,4096]{1,0:T(8,128)} fusion(bf16[1,1,4096,768]{3,2,1,0:T(8,128)(2,1)} %param.17, f32[288,768]{1,0:T(8,128)} %fusion.28, bf16[288,4096]{1,0:T(8,128)(2,1)} %reshape.254, bf16[1,1,4096,768]{3,2,1,0:T(8,128)(2,1)} %param.18, f32[288,768]{1,0:T(8,128)} %fusion.10), kind=kOutput, calls=%fused_computation.20 | convolution fusion | flops 3626090496 | bytes 21430272 | tf_op jit(solution)/shard_map/dot_general | solution.py:20
  131.9 8.1 %fusion.45 = bf16[288,4096]{1,0:T(8,128)(2,1)} fusion(f32[288,4096]{1,0:T(8,128)} %fusion.8, bf16[1,1,4096,768]{3,2,1,0:T(8,128)(2,1)} %param.18, f32[288,768]{1,0:T(8,128)} %fusion.28, f32[288,768]{1,0:T(8,128)} %fusion.10), kind=kOutput, calls=%fused_computation.47 | convolution fusion | flops 1815625728 | bytes 15138816 | tf_op jit(solution)/shard_map/dot_general | solution.py:21
  149.2 32.2 %all-to-all-done.2 = bf16[8,36,4096]{2,1,0:T(8,128)(2,1)} async-done(((bf16[8,36,4096]{2,1,0:T(8,128)(2,1)}), bf16[8,36,4096]{2,1,0:T(8,128)(2,1)}, u32[]{:S(2)}, u32[]{:S(2)}) %all-to-all-start.2) | async-done | bytes 2359328 | tf_op jit(solution)/shard_map/all_to_all | solution.py:72
  185.5 7.2 %gather_fusion.2 = bf16[256,4096]{1,0:T(8,128)(2,1)} fusion(bf16[288,4096]{1,0:T(8,128)(2,1)} %reshape.256, s32[1024]{0:T(1024)S(1)} %pad_clamp_fusion.4), kind=kCustom, calls=%fused_computation.1.clone | custom fusion | bytes 4195328 | tf_op jit(solution)/shard_map/jit(_take)/gather | solution.py:73
  197.5 10.8 %multiply_reduce_fusion.2 = f32[128,4096]{1,0:T(8,128)S(1)} fusion(bf16[128,2,4096]{2,1,0:T(2,128)(2,1)} %reshape.384, pred[128,2]{1,0:T(8,128)(4,1)S(1)} %copy.16, f32[128,2]{1,0:T(8,128)S(1)} %copy.15), kind=kLoop, calls=%fused_computation.50 | loop fusion | flops 3670016 | bytes 4195584 | tf_op jit(solution)/shard_map/reduce_sum | solution.py:76
  216.0 10.2 %collective-permute-done = bf16[128,4096]{1,0:T(8,128)(2,1)S(1)} collective-permute-done((bf16[128,4096]{1,0:T(8,128)(2,1)}, bf16[128,4096]{1,0:T(8,128)(2,1)S(1)}, u32[]{:S(2)}, u32[]{:S(2)}) %collective-permute-start) | collective-permute-done | bytes 1048608 | tf_op jit(solution)/shard_map/ppermute | solution.py:9
  239.0 8.6 %all-to-all-start.3 = ((bf16[8,36,4096]{2,1,0:T(8,128)(2,1)}), bf16[8,36,4096]{2,1,0:T(8,128)(2,1)}, u32[]{:S(2)}, u32[]{:S(2)}) async-start(bf16[8,36,4096]{2,1,0:T(8,128)(2,1)} %reshape.257), calls=%async_computation.3 | async-start | bytes 5242880 | tf_op jit(solution)/shard_map/all_to_all | solution.py:61
  251.8 28.6 %all-to-all-done.3 = bf16[8,36,4096]{2,1,0:T(8,128)(2,1)} async-done(((bf16[8,36,4096]{2,1,0:T(8,128)(2,1)}), bf16[8,36,4096]{2,1,0:T(8,128)(2,1)}, u32[]{:S(2)}, u32[]{:S(2)}) %all-to-all-start.3) | async-done | bytes 2359328 | tf_op jit(solution)/shard_map/all_to_all | solution.py:61
  280.4 6.7 %all-to-all-start.4 = ((bf16[8,36,4096]{2,1,0:T(8,128)(2,1)}), bf16[8,36,4096]{2,1,0:T(8,128)(2,1)}, u32[]{:S(2)}, u32[]{:S(2)}) async-start(bf16[8,36,4096]{2,1,0:T(8,128)(2,1)} %reshape.259), calls=%async_computation.4 | async-start | bytes 5242880 | tf_op jit(solution)/shard_map/all_to_all | solution.py:62
  296.7 23.1 %all-to-all-done.4 = bf16[8,36,4096]{2,1,0:T(8,128)(2,1)} async-done(((bf16[8,36,4096]{2,1,0:T(8,128)(2,1)}), bf16[8,36,4096]{2,1,0:T(8,128)(2,1)}, u32[]{:S(2)}, u32[]{:S(2)}) %all-to-all-start.4) | async-done | bytes 2359328 | tf_op jit(solution)/shard_map/all_to_all | solution.py:62
  330.4 12.8 %fusion.4 = f32[288,4096]{1,0:T(8,128)} fusion(bf16[1,1,4096,768]{3,2,1,0:T(8,128)(2,1)} %param.17, f32[288,768]{1,0:T(8,128)S(1)} %fusion.26, bf16[288,4096]{1,0:T(8,128)(2,1)} %reshape.260, bf16[1,1,4096,768]{3,2,1,0:T(8,128)(2,1)} %param.18, f32[288,768]{1,0:T(8,128)} %fusion.6), kind=kOutput, calls=%fused_computation.16 | convolution fusion | flops 3626090496 | bytes 21430272 | tf_op jit(solution)/shard_map/dot_general | solution.py:20
  343.1 7.9 %fusion.42 = bf16[288,4096]{1,0:T(8,128)(2,1)} fusion(f32[288,4096]{1,0:T(8,128)} %fusion.4, bf16[1,1,4096,768]{3,2,1,0:T(8,128)(2,1)} %param.18, f32[288,768]{1,0:T(8,128)S(1)} %fusion.26, f32[288,768]{1,0:T(8,128)} %fusion.6), kind=kOutput, calls=%fused_computation.46 | convolution fusion | flops 1815625728 | bytes 15138816 | tf_op jit(solution)/shard_map/dot_general | solution.py:21
  360.4 32.2 %all-to-all-done.5 = bf16[8,36,4096]{2,1,0:T(8,128)(2,1)} async-done(((bf16[8,36,4096]{2,1,0:T(8,128)(2,1)}), bf16[8,36,4096]{2,1,0:T(8,128)(2,1)}, u32[]{:S(2)}, u32[]{:S(2)}) %all-to-all-start.5) | async-done | bytes 2359328 | tf_op jit(solution)/shard_map/all_to_all | solution.py:72
  396.8 7.2 %gather_fusion.5 = bf16[256,4096]{1,0:T(8,128)(2,1)} fusion(bf16[288,4096]{1,0:T(8,128)(2,1)} %reshape.262, s32[1024]{0:T(1024)S(1)} %pad_clamp_fusion.2), kind=kCustom, calls=%fused_computation.7.clone | custom fusion | bytes 4195328 | tf_op jit(solution)/shard_map/jit(_take)/gather | solution.py:73
  408.4 10.8 %multiply_reduce_fusion.1 = f32[128,4096]{1,0:T(8,128)S(1)} fusion(bf16[128,2,4096]{2,1,0:T(2,128)(2,1)} %reshape.392, pred[128,2]{1,0:T(8,128)(4,1)S(1)} %copy.20, f32[128,2]{1,0:T(8,128)S(1)} %copy.19), kind=kLoop, calls=%fused_computation.49 | loop fusion | flops 3670016 | bytes 4195584 | tf_op jit(solution)/shard_map/reduce_sum | solution.py:76
  426.8 16.3 %collective-permute-done.1 = bf16[128,4096]{1,0:T(8,128)(2,1)S(1)} collective-permute-done((bf16[128,4096]{1,0:T(8,128)(2,1)}, bf16[128,4096]{1,0:T(8,128)(2,1)S(1)}, u32[]{:S(2)}, u32[]{:S(2)}) %collective-permute-start.1) | collective-permute-done | bytes 1048608 | tf_op jit(solution)/shard_map/ppermute | solution.py:9
  456.0 9.3 %all-to-all-start.7 = ((bf16[8,36,4096]{2,1,0:T(8,128)(2,1)}), bf16[8,36,4096]{2,1,0:T(8,128)(2,1)}, u32[]{:S(2)}, u32[]{:S(2)}) async-start(bf16[8,36,4096]{2,1,0:T(8,128)(2,1)} %reshape.265), calls=%async_computation.7 | async-start | bytes 5242880 | tf_op jit(solution)/shard_map/all_to_all | solution.py:62
  469.4 23.3 %all-to-all-done.7 = bf16[8,36,4096]{2,1,0:T(8,128)(2,1)} async-done(((bf16[8,36,4096]{2,1,0:T(8,128)(2,1)}), bf16[8,36,4096]{2,1,0:T(8,128)(2,1)}, u32[]{:S(2)}, u32[]{:S(2)}) %all-to-all-start.7) | async-done | bytes 2359328 | tf_op jit(solution)/shard_map/all_to_all | solution.py:62
  506.8 23.2 %all-to-all-done.6 = bf16[8,36,4096]{2,1,0:T(8,128)(2,1)} async-done(((bf16[8,36,4096]{2,1,0:T(8,128)(2,1)}), bf16[8,36,4096]{2,1,0:T(8,128)(2,1)}, u32[]{:S(2)}, u32[]{:S(2)}) %all-to-all-start.6) | async-done | bytes 2359328 | tf_op jit(solution)/shard_map/all_to_all | solution.py:61
  539.6 12.5 %fusion = f32[288,4096]{1,0:T(8,128)} fusion(bf16[1,1,4096,768]{3,2,1,0:T(8,128)(2,1)} %param.17, f32[288,768]{1,0:T(8,128)S(1)} %fusion.24, bf16[288,4096]{1,0:T(8,128)(2,1)} %reshape.266, bf16[1,1,4096,768]{3,2,1,0:T(8,128)(2,1)} %param.18, f32[288,768]{1,0:T(8,128)S(1)} %fusion.2), kind=kOutput, calls=%fused_computation.12 | convolution fusion | flops 3626090496 | bytes 21430272 | tf_op jit(solution)/shard_map/dot_general | solution.py:20
  552.1 7.6 %fusion.39 = bf16[288,4096]{1,0:T(8,128)(2,1)} fusion(f32[288,4096]{1,0:T(8,128)} %fusion, bf16[1,1,4096,768]{3,2,1,0:T(8,128)(2,1)} %param.18, f32[288,768]{1,0:T(8,128)S(1)} %fusion.24, f32[288,768]{1,0:T(8,128)S(1)} %fusion.2), kind=kOutput, calls=%fused_computation.45 | convolution fusion | flops 1815625728 | bytes 15138816 | tf_op jit(solution)/shard_map/dot_general | solution.py:21
  563.9 10.9 %all-to-all-start.8 = ((bf16[8,36,4096]{2,1,0:T(8,128)(2,1)}), bf16[8,36,4096]{2,1,0:T(8,128)(2,1)}, u32[]{:S(2)}, u32[]{:S(2)}) async-start(bf16[8,36,4096]{2,1,0:T(8,128)(2,1)} %reshape.267), calls=%async_computation.8 | async-start | bytes 5242880 | tf_op jit(solution)/shard_map/all_to_all | solution.py:72
  575.3 32.2 %all-to-all-done.8 = bf16[8,36,4096]{2,1,0:T(8,128)(2,1)} async-done(((bf16[8,36,4096]{2,1,0:T(8,128)(2,1)}), bf16[8,36,4096]{2,1,0:T(8,128)(2,1)}, u32[]{:S(2)}, u32[]{:S(2)}) %all-to-all-start.8) | async-done | bytes 2359328 | tf_op jit(solution)/shard_map/all_to_all | solution.py:72
  611.7 7.2 %gather_fusion.8 = bf16[256,4096]{1,0:T(8,128)(2,1)} fusion(bf16[288,4096]{1,0:T(8,128)(2,1)} %reshape.268, s32[1024]{0:T(1024)S(1)} %pad_clamp_fusion), kind=kCustom, calls=%fused_computation.8.clone | custom fusion | bytes 4195328 | tf_op jit(solution)/shard_map/jit(_take)/gather | solution.py:73
  623.3 10.8 %multiply_reduce_fusion = f32[128,4096]{1,0:T(8,128)S(1)} fusion(bf16[128,2,4096]{2,1,0:T(2,128)(2,1)} %reshape.400, pred[128,2]{1,0:T(8,128)(4,1)S(1)} %copy.24, f32[128,2]{1,0:T(8,128)S(1)} %copy.23), kind=kLoop, calls=%fused_computation.48 | loop fusion | flops 3670016 | bytes 4195584 | tf_op jit(solution)/shard_map/reduce_sum | solution.py:76
  635.2 22.0 %collective-permute-done.2 = bf16[128,4096]{1,0:T(8,128)(2,1)S(1)} collective-permute-done((bf16[128,4096]{1,0:T(8,128)(2,1)S(1)}, bf16[128,4096]{1,0:T(8,128)(2,1)S(1)}, u32[]{:S(2)}, u32[]{:S(2)}) %collective-permute-start.2) | collective-permute-done | bytes 1048608 | tf_op jit(solution)/shard_map/ppermute | solution.py:9
  (93 shorter events, 182.3 us)
Async XLA Ops:
  6.3 9.4 %copy-start = (bf16[1,128,4096]{2,1,0:T(8,128)(2,1)S(1)}, bf16[1,128,4096]{2,1,0:T(8,128)(2,1)}, u32[]{:S(2)}) copy-start(bf16[1,128,4096]{2,1,0:T(8,128)(2,1)} %param.12) | copy-start | bytes 3145732
  28.6 39.1 %all-to-all-start.1 = ((bf16[8,36,4096]{2,1,0:T(8,128)(2,1)}), bf16[8,36,4096]{2,1,0:T(8,128)(2,1)}, u32[]{:S(2)}, u32[]{:S(2)}) async-start(bf16[8,36,4096]{2,1,0:T(8,128)(2,1)} %reshape.253), calls=%async_computation.1 | async-start | bytes 5242880 | tf_op jit(solution)/shard_map/all_to_all | solution.py:62
  67.8 40.6 %all-to-all-start = ((bf16[8,36,4096]{2,1,0:T(8,128)(2,1)}), bf16[8,36,4096]{2,1,0:T(8,128)(2,1)}, u32[]{:S(2)}, u32[]{:S(2)}) async-start(bf16[8,36,4096]{2,1,0:T(8,128)(2,1)} %reshape.251), calls=%async_computation | async-start | bytes 5242880 | tf_op jit(solution)/shard_map/all_to_all | solution.py:61
  144.1 4.9 copy-start.1
  144.1 37.2 %all-to-all-start.2 = ((bf16[8,36,4096]{2,1,0:T(8,128)(2,1)}), bf16[8,36,4096]{2,1,0:T(8,128)(2,1)}, u32[]{:S(2)}, u32[]{:S(2)}) async-start(bf16[8,36,4096]{2,1,0:T(8,128)(2,1)} %reshape.255), calls=%async_computation.2 | async-start | bytes 5242880 | tf_op jit(solution)/shard_map/all_to_all | solution.py:72
  209.5 16.7 %collective-permute-start = (bf16[128,4096]{1,0:T(8,128)(2,1)}, bf16[128,4096]{1,0:T(8,128)(2,1)S(1)}, u32[]{:S(2)}, u32[]{:S(2)}) collective-permute-start(bf16[128,4096]{1,0:T(8,128)(2,1)} %add_convert_fusion.2), channel_id=1, source_target_pairs={{0,120},{8,0},{16,8},{24,16},{32,24},{40,32},{48,40},{56,48},{64,5... | collective-permute-start | bytes 3145736 | tf_op jit(solution)/shard_map/ppermute | solution.py:9
  239.0 41.4 %all-to-all-start.3 = ((bf16[8,36,4096]{2,1,0:T(8,128)(2,1)}), bf16[8,36,4096]{2,1,0:T(8,128)(2,1)}, u32[]{:S(2)}, u32[]{:S(2)}) async-start(bf16[8,36,4096]{2,1,0:T(8,128)(2,1)} %reshape.257), calls=%async_computation.3 | async-start | bytes 5242880 | tf_op jit(solution)/shard_map/all_to_all | solution.py:61
  280.4 39.4 %all-to-all-start.4 = ((bf16[8,36,4096]{2,1,0:T(8,128)(2,1)}), bf16[8,36,4096]{2,1,0:T(8,128)(2,1)}, u32[]{:S(2)}, u32[]{:S(2)}) async-start(bf16[8,36,4096]{2,1,0:T(8,128)(2,1)} %reshape.259), calls=%async_computation.4 | async-start | bytes 5242880 | tf_op jit(solution)/shard_map/all_to_all | solution.py:62
  355.1 37.6 %all-to-all-start.5 = ((bf16[8,36,4096]{2,1,0:T(8,128)(2,1)}), bf16[8,36,4096]{2,1,0:T(8,128)(2,1)}, u32[]{:S(2)}, u32[]{:S(2)}) async-start(bf16[8,36,4096]{2,1,0:T(8,128)(2,1)} %reshape.261), calls=%async_computation.5 | async-start | bytes 5242880 | tf_op jit(solution)/shard_map/all_to_all | solution.py:72
  420.4 22.7 %collective-permute-start.1 = (bf16[128,4096]{1,0:T(8,128)(2,1)}, bf16[128,4096]{1,0:T(8,128)(2,1)S(1)}, u32[]{:S(2)}, u32[]{:S(2)}) collective-permute-start(bf16[128,4096]{1,0:T(8,128)(2,1)} %add_convert_fusion.1), channel_id=1, source_target_pairs={{0,120},{8,0},{16,8},{24,16},{32,24},{40,32},{48,40},{56,48},{64,5... | collective-permute-start | bytes 3145736 | tf_op jit(solution)/shard_map/ppermute | solution.py:9
  456.0 36.8 %all-to-all-start.7 = ((bf16[8,36,4096]{2,1,0:T(8,128)(2,1)}), bf16[8,36,4096]{2,1,0:T(8,128)(2,1)}, u32[]{:S(2)}, u32[]{:S(2)}) async-start(bf16[8,36,4096]{2,1,0:T(8,128)(2,1)} %reshape.265), calls=%async_computation.7 | async-start | bytes 5242880 | tf_op jit(solution)/shard_map/all_to_all | solution.py:62
  492.8 37.2 %all-to-all-start.6 = ((bf16[8,36,4096]{2,1,0:T(8,128)(2,1)}), bf16[8,36,4096]{2,1,0:T(8,128)(2,1)}, u32[]{:S(2)}, u32[]{:S(2)}) async-start(bf16[8,36,4096]{2,1,0:T(8,128)(2,1)} %reshape.263), calls=%async_computation.6 | async-start | bytes 5242880 | tf_op jit(solution)/shard_map/all_to_all | solution.py:61
  563.9 11.2 %copy-start.2 = (pred[128,2]{0,1:T(4,128)(4,1)S(1)}, pred[128,2]{0,1:T(4,128)(4,1)}, u32[]{:S(2)}) copy-start(pred[128,2]{0,1:T(4,128)(4,1)} %get-tuple-element.6) | copy-start | bytes 772
  563.9 43.7 %all-to-all-start.8 = ((bf16[8,36,4096]{2,1,0:T(8,128)(2,1)}), bf16[8,36,4096]{2,1,0:T(8,128)(2,1)}, u32[]{:S(2)}, u32[]{:S(2)}) async-start(bf16[8,36,4096]{2,1,0:T(8,128)(2,1)} %reshape.267), calls=%async_computation.8 | async-start | bytes 5242880 | tf_op jit(solution)/shard_map/all_to_all | solution.py:72
  634.3 22.9 %collective-permute-start.2 = (bf16[128,4096]{1,0:T(8,128)(2,1)S(1)}, bf16[128,4096]{1,0:T(8,128)(2,1)S(1)}, u32[]{:S(2)}, u32[]{:S(2)}) collective-permute-start(bf16[128,4096]{1,0:T(8,128)(2,1)S(1)} %add_convert_fusion), channel_id=1, source_target_pairs={{0,120},{8,0},{16,8},{24,16},{32,24},{40,32},{48,40},{56,48},{64,5... | collective-permute-start | bytes 3145736 | tf_op jit(solution)/shard_map/ppermute | solution.py:9
where the time goes:
time: 671 us; the launch traced here: 658 us
  waiting for transfers between devices  294 us (44%)
  local copies, waits for them, and re-layouts  149 us (22%)
  matrix products  97.7 us (15%)
  starting transfers between devices  66 us (10%)
  other arithmetic  51.3 us (8%)
    all_to_all x3, waiting for transfers between devices, per_device(): lax.all_to_all(returned, 'expert', split_axis=0, concat_axis=0, tiled=True)  96.6 us
    all_to_all x3, waiting for transfers between devices, per_device(): lax.all_to_all(input_buffer, 'expert', split_axis=0, concat_axis=0, tiled...  75.1 us
    all_to_all x3, waiting for transfers between devices, per_device(): lax.all_to_all(grad_buffer, 'expert', split_axis=0, concat_axis=0, tiled=...  74 us
    ppermute x3, waiting for transfers between devices, shifted(): lax.ppermute(x, axis, [(i, (i + by) % devices) for i in range(devices)])  48.5 us
    dot_general x3, matrix products, expert_pass(): summed = jnp.dot(grad_gate, gate_proj.T, preferred_element_type=jnp.float32)  38.3 us
    gather x6, local copies, waits for them, and re-layouts, per_device(): jnp.take(arrived.reshape(groups * capacity, width), positions, axis=0, mo...  35.2 us
    reduce_sum x3, other arithmetic, per_device(): jnp.sum(gates[step, 0][..., None] * picked.astype(jnp.float32), axis=1)  32.4 us
    gather x6, local copies, waits for them, and re-layouts, collect(): jnp.take(rows, sources, axis=0, mode='fill', fill_value=0)  28.6 us
  transfers between devices with their start and end apart: 12, of which 12 were waited for; matrix products, arithmetic and copies ran while one was open for 8% of the time, Pallas kernels for 0%

commit v1 on v0

v1 whole, which is shorter than its diff:
```python
import jax
import jax.numpy as jnp
from jax import lax
from jax.sharding import PartitionSpec as P


def shifted(x, axis, by):
    devices = lax.axis_size(axis)
    return lax.ppermute(x, axis, [(i, (i + by) % devices) for i in range(devices)])


def forward_part(input_part, gate_proj, up_proj):
    pre_gate = jnp.dot(input_part, gate_proj, preferred_element_type=jnp.float32)
    pre_up = jnp.dot(input_part, up_proj, preferred_element_type=jnp.float32)
    return pre_gate, pre_up


def backward_part(grad_part, pre_gate, pre_up, gate_proj, up_proj, down_proj):
    grad_hidden = jnp.dot(grad_part, down_proj.T, preferred_element_type=jnp.float32)
    sigma = jax.nn.sigmoid(pre_gate)
    derivative = sigma * (1.0 + pre_gate * (1.0 - sigma))
    grad_gate = (grad_hidden * pre_up * derivative).astype(jnp.bfloat16)
    grad_up = (grad_hidden * pre_gate * sigma).astype(jnp.bfloat16)
    summed = jnp.dot(grad_gate, gate_proj.T, preferred_element_type=jnp.float32)
    summed = summed + jnp.dot(grad_up, up_proj.T, preferred_element_type=jnp.float32)
    return summed.astype(jnp.bfloat16)


def per_device(grad_in, saved_inputs, expert_ids, slots, gates, w_gate, w_up, w_down):
    groups = lax.axis_size("expert")
    rows_dev = grad_in.shape[1]
    width = grad_in.shape[2]
    rounds = saved_inputs.shape[0]
    capacity = 9 * rows_dev * expert_ids.shape[-1] // (8 * groups)
    padded = -(-capacity // 16) * 16
    columns = groups * padded
    gate_proj = w_gate[0, 0]
    up_proj = w_up[0, 0]
    down_proj = w_down[0, 0]
    column_ids = jnp.arange(columns, dtype=jnp.int32)

    def route_plan(step):
        route_ids = expert_ids[step, 0]
        slot_ids = slots[step, 0]
        target = jnp.where(slot_ids < capacity, route_ids * padded + slot_ids, -1)
        hit = target[:, :, None] == column_ids[None, None, :]
        dispatch = jnp.any(hit, axis=1).T.astype(jnp.bfloat16)
        weights = jnp.sum(jnp.where(hit, gates[step, 0][:, :, None], 0.0), axis=1)
        weights_hi = weights.astype(jnp.bfloat16)
        weights_lo = (weights - weights_hi.astype(jnp.float32)).astype(jnp.bfloat16)
        return dispatch, weights_hi, weights_lo

    def collect(dispatch, rows):
        picked = jnp.dot(dispatch, rows, preferred_element_type=jnp.float32)
        return picked.astype(jnp.bfloat16).reshape(groups, padded, width)

    def exchange(buffer):
        moved = lax.all_to_all(buffer, "expert", split_axis=0, concat_axis=0, tiled=True)
        return moved.reshape(columns, width)

    plans = [route_plan(step) for step in range(rounds)]
    forwards = []
    for step in range(rounds):
        input_part = exchange(collect(plans[step][0], saved_inputs[step, 0]))
        forwards.append(forward_part(input_part, gate_proj, up_proj))

    present_block = grad_in[0]
    for step in range(rounds):
        dispatch, weights_hi, weights_lo = plans[step]
        grad_part = exchange(collect(dispatch, present_block))
        pre_gate, pre_up = forwards[step]
        result = backward_part(grad_part, pre_gate, pre_up, gate_proj, up_proj, down_proj)
        arrived = exchange(result.reshape(groups, padded, width))
        combined = jnp.dot(weights_hi, arrived, preferred_element_type=jnp.float32)
        combined = combined + jnp.dot(weights_lo, arrived, preferred_element_type=jnp.float32)
        summed = present_block.astype(jnp.float32) + combined
        present_block = shifted(summed.astype(jnp.bfloat16), "section", -1)
    return present_block[None]


def solution(mesh):
    placed = (
        P("section", "expert", None),
        P(None, "section", "expert", None),
        P(None, "section", "expert", None),
        P(None, "section", "expert", None),
        P(None, "section", "expert", None),
        P("section", "expert", None, None),
        P("section", "expert", None, None),
        P("section", "expert", None, None),
    )
    return jax.shard_map(
        per_device,
        mesh=mesh,
        in_specs=placed,
        out_specs=P("section", "expert", None),
        check_vma=False,
    )
```

time: 671 us -> 573 us (0.85)
  local copies, waits for them, and re-layouts: 149 us -> 4.14 us
  other arithmetic: 51.3 us -> 1.47 us
  matrix products: 97.7 us -> 141 us
  waiting for transfers between devices: 294 us -> 332 us
  starting transfers between devices: 66 us -> 82.9 us
    reshape x19 -> x0, local copies, waits for them, and re-layouts: 74.4 us -> none  [the longest x6 24.8 us: collect(): jnp.take(rows, sources, axis=0, mode='fill', fill_value=0)]
    gather x12 -> x0, local copies, waits for them, and re-layouts: 63.8 us -> none  [the longest x6 35.2 us: per_device(): jnp.take(arrived.reshape(groups * capacity, width), positions, axis=0, mo...]
    ppermute x3, waiting for transfers between devices: 48.5 us -> 94.2 us  [shifted(): lax.ppermute(x, axis, [(i, (i + by) % devices) for i in range(devices)])]
    dot_general x12 -> x24, matrix products: 97.7 us -> 141 us  [the longest x3 47 us: backward_part(): summed = jnp.dot(grad_gate, gate_proj.T, preferred_element_type=jnp.float32)]
    reduce_sum x3, other arithmetic: 32.4 us -> 0.4 us  [route_plan(): weights = jnp.sum(jnp.where(hit, gates[step, 0][:, :, None], 0.0), axis=1)]
    all_to_all x9, starting transfers between devices: 63.5 us -> 77.9 us  [exchange(): lax.all_to_all(buffer, 'expert', split_axis=0, concat_axis=0, tiled=True)]
    select_n x11 -> x1, other arithmetic: 14.9 us -> 0.77 us  [route_plan(): target = jnp.where(slot_ids < capacity, route_ids * padded + slot_ids, -1)]
    all_to_all x9, waiting for transfers between devices: 246 us -> 238 us  [exchange(): lax.all_to_all(buffer, 'expert', split_axis=0, concat_axis=0, tiled=True)]
  transfers between devices with their start and end apart: 12 -> 12, of which waited for: 12 -> 11; matrix products, arithmetic and copies ran while one was open for 8% -> 7% of each run, Pallas kernels for 0% -> 0%
where the time goes in v1:
time: 573 us; the launch traced here: 562 us
  waiting for transfers between devices  332 us (58%)
  matrix products  141 us (25%)
  starting transfers between devices  82.9 us (14%)
    all_to_all x9, waiting for transfers between devices, exchange(): lax.all_to_all(buffer, 'expert', split_axis=0, concat_axis=0, tiled=True)  238 us
    ppermute x3, waiting for transfers between devices, shifted(): lax.ppermute(x, axis, [(i, (i + by) % devices) for i in range(devices)])  94.2 us
    all_to_all x9, starting transfers between devices, exchange(): lax.all_to_all(buffer, 'expert', split_axis=0, concat_axis=0, tiled=True)  77.9 us
    dot_general x3, matrix products, backward_part(): summed = jnp.dot(grad_gate, gate_proj.T, preferred_element_type=jnp.float32)  47 us
    dot_general x3, matrix products, backward_part(): jnp.dot(grad_up, up_proj.T, preferred_element_type=jnp.float32)  28.1 us
    dot_general x3, matrix products, forward_part(): jnp.dot(input_part, gate_proj, preferred_element_type=jnp.float32)  22.1 us
    dot_general x6, matrix products, collect(): picked = jnp.dot(dispatch, rows, preferred_element_type=jnp.float32)  19.8 us
    dot_general x3, matrix products, backward_part(): jnp.dot(grad_part, down_proj.T, preferred_element_type=jnp.float32)  19.3 us
  transfers between devices with their start and end apart: 12, of which 11 were waited for; matrix products, arithmetic and copies ran while one was open for 7% of the time, Pallas kernels for 0%

profile of v1, /device:TPU:1, one launch (start us, length us, event | category | flops | bytes accessed | tf_op | source)
XLA Modules:
  0.0 562.2 jit_solution(2705466167640925295)
XLA Ops:
  0.9 3.9 convolution_convert_fusion.4
  4.8 6.5 %all-to-all-start.1 = ((bf16[8,48,4096]{2,1,0:T(8,128)(2,1)}), bf16[8,48,4096]{2,1,0:T(8,128)(2,1)}, u32[]{:S(2)}, u32[]{:S(2)}) async-start(bf16[8,48,4096]{2,1,0:T(8,128)(2,1)} %bitcast.7), calls=%async_computation.1 | async-start | bytes 6291456 | tf_op jit(solution)/shard_map/all_to_all | solution.py:58
  14.0 35.7 %all-to-all-done.1 = bf16[8,48,4096]{2,1,0:T(8,128)(2,1)} async-done(((bf16[8,48,4096]{2,1,0:T(8,128)(2,1)}), bf16[8,48,4096]{2,1,0:T(8,128)(2,1)}, u32[]{:S(2)}, u32[]{:S(2)}) %all-to-all-start.1) | async-done | bytes 3145760 | tf_op jit(solution)/shard_map/all_to_all | solution.py:58
  49.7 10.6 %all-to-all-start = ((bf16[8,48,4096]{2,1,0:T(8,128)(2,1)}), bf16[8,48,4096]{2,1,0:T(8,128)(2,1)S(1)}, u32[]{:S(2)}, u32[]{:S(2)}) async-start(bf16[8,48,4096]{2,1,0:T(8,128)(2,1)} %bitcast.3), calls=%async_computation | async-start | bytes 6291456 | tf_op jit(solution)/shard_map/all_to_all | solution.py:58
  60.3 7.4 %fusion.10 = f32[384,768]{1,0:T(8,128)} fusion(bf16[384,4096]{1,0:T(8,128)(2,1)} %bitcast.8, bf16[1,1,4096,768]{3,2,1,0:T(8,128)(2,1)} %param.13), kind=kOutput, calls=%fused_computation.10 | convolution fusion | flops 2415919104 | bytes 10616832 | tf_op jit(solution)/shard_map/dot_general | solution.py:13
  67.7 30.9 %all-to-all-done = bf16[8,48,4096]{2,1,0:T(8,128)(2,1)S(1)} async-done(((bf16[8,48,4096]{2,1,0:T(8,128)(2,1)}), bf16[8,48,4096]{2,1,0:T(8,128)(2,1)S(1)}, u32[]{:S(2)}, u32[]{:S(2)}) %all-to-all-start) | async-done | bytes 3145760 | tf_op jit(solution)/shard_map/all_to_all | solution.py:58
  98.6 6.4 %fusion.28 = f32[384,768]{1,0:T(8,128)} fusion(bf16[384,4096]{1,0:T(8,128)(2,1)S(1)} %bitcast.139, bf16[1,1,768,4096]{3,2,1,0:T(8,128)(2,1)} %param.15), kind=kOutput, calls=%fused_computation.28 | convolution fusion | flops 2415919104 | bytes 10616832 | tf_op jit(solution)/shard_map/dot_general | solution.py:19
  105.0 15.7 %fusion.8 = f32[384,4096]{1,0:T(8,128)} fusion(bf16[1,1,4096,768]{3,2,1,0:T(8,128)(2,1)} %param.13, f32[384,768]{1,0:T(8,128)} %fusion.28, bf16[384,4096]{1,0:T(8,128)(2,1)} %bitcast.8, bf16[1,1,4096,768]{3,2,1,0:T(8,128)(2,1)} %param.14, f32[384,768]{1,0:T(8,128)} %fusion.10), kind=kOutput, calls=%fused_computation.8 | convolution fusion | flops 4834787328 | bytes 24379392 | tf_op jit(solution)/shard_map/dot_general | solution.py:24
  120.7 9.4 %add_convert_fusion.2 = bf16[384,4096]{1,0:T(8,128)(2,1)} fusion(f32[384,4096]{1,0:T(8,128)} %fusion.8, bf16[1,1,4096,768]{3,2,1,0:T(8,128)(2,1)} %param.14, f32[384,768]{1,0:T(8,128)S(1)} %copy-done.10, f32[384,768]{1,0:T(8,128)S(1)} %copy-done.7), kind=kOutput, calls=%fused_computation.32 | convolution fusion | flops 2420834304 | bytes 18087936 | tf_op jit(solution)/shard_map/dot_general | solution.py:25
  130.1 4.7 all-to-all-start.2
  138.8 34.3 %all-to-all-done.2 = bf16[8,48,4096]{2,1,0:T(8,128)(2,1)S(1)} async-done(((bf16[8,48,4096]{2,1,0:T(8,128)(2,1)}), bf16[8,48,4096]{2,1,0:T(8,128)(2,1)S(1)}, u32[]{:S(2)}, u32[]{:S(2)}) %all-to-all-start.2) | async-done | bytes 3145760 | tf_op jit(solution)/shard_map/all_to_all | solution.py:58
  173.0 4.9 all-to-all-start.4
  180.8 46.4 %collective-permute-done = bf16[128,4096]{1,0:T(8,128)(2,1)S(1)} collective-permute-done((bf16[128,4096]{1,0:T(8,128)(2,1)S(1)}, bf16[128,4096]{1,0:T(8,128)(2,1)S(1)}, u32[]{:S(2)}, u32[]{:S(2)}) %collective-permute-start) | collective-permute-done | bytes 1048608 | tf_op jit(solution)/shard_map/ppermute | solution.py:9
  230.9 4.5 all-to-all-start.3
  235.4 7.4 %fusion.6 = f32[384,768]{1,0:T(8,128)} fusion(bf16[384,4096]{1,0:T(8,128)(2,1)} %bitcast.19, bf16[1,1,4096,768]{3,2,1,0:T(8,128)(2,1)} %param.13), kind=kOutput, calls=%fused_computation.6 | convolution fusion | flops 2415919104 | bytes 10616832 | tf_op jit(solution)/shard_map/dot_general | solution.py:13
  242.8 30.9 %all-to-all-done.3 = bf16[8,48,4096]{2,1,0:T(8,128)(2,1)S(1)} async-done(((bf16[8,48,4096]{2,1,0:T(8,128)(2,1)}), bf16[8,48,4096]{2,1,0:T(8,128)(2,1)S(1)}, u32[]{:S(2)}, u32[]{:S(2)}) %all-to-all-start.3) | async-done | bytes 3145760 | tf_op jit(solution)/shard_map/all_to_all | solution.py:58
  273.8 6.4 %fusion.26 = f32[384,768]{1,0:T(8,128)} fusion(bf16[384,4096]{1,0:T(8,128)(2,1)S(1)} %bitcast.140, bf16[1,1,768,4096]{3,2,1,0:T(8,128)(2,1)} %param.15), kind=kOutput, calls=%fused_computation.26 | convolution fusion | flops 2415919104 | bytes 10616832 | tf_op jit(solution)/shard_map/dot_general | solution.py:19
  280.2 15.7 %fusion.4 = f32[384,4096]{1,0:T(8,128)} fusion(bf16[1,1,4096,768]{3,2,1,0:T(8,128)(2,1)} %param.13, f32[384,768]{1,0:T(8,128)} %fusion.26, bf16[384,4096]{1,0:T(8,128)(2,1)} %bitcast.19, bf16[1,1,4096,768]{3,2,1,0:T(8,128)(2,1)} %param.14, f32[384,768]{1,0:T(8,128)} %fusion.6), kind=kOutput, calls=%fused_computation.4 | convolution fusion | flops 4834787328 | bytes 24379392 | tf_op jit(solution)/shard_map/dot_general | solution.py:24
  295.9 9.4 %add_convert_fusion.1 = bf16[384,4096]{1,0:T(8,128)(2,1)} fusion(f32[384,4096]{1,0:T(8,128)} %fusion.4, bf16[1,1,4096,768]{3,2,1,0:T(8,128)(2,1)} %param.14, f32[384,768]{1,0:T(8,128)S(1)} %copy-done.11, f32[384,768]{1,0:T(8,128)S(1)} %copy-done.8), kind=kOutput, calls=%fused_computation.31 | convolution fusion | flops 2420834304 | bytes 18087936 | tf_op jit(solution)/shard_map/dot_general | solution.py:25
  305.3 12.0 %all-to-all-start.5 = ((bf16[8,48,4096]{2,1,0:T(8,128)(2,1)}), bf16[8,48,4096]{2,1,0:T(8,128)(2,1)S(1)}, u32[]{:S(2)}, u32[]{:S(2)}) async-start(bf16[8,48,4096]{2,1,0:T(8,128)(2,1)} %bitcast.141), calls=%async_computation.5 | async-start | bytes 6291456 | tf_op jit(solution)/shard_map/all_to_all | solution.py:58
  321.3 34.3 %all-to-all-done.5 = bf16[8,48,4096]{2,1,0:T(8,128)(2,1)S(1)} async-done(((bf16[8,48,4096]{2,1,0:T(8,128)(2,1)}), bf16[8,48,4096]{2,1,0:T(8,128)(2,1)S(1)}, u32[]{:S(2)}, u32[]{:S(2)}) %all-to-all-start.5) | async-done | bytes 3145760 | tf_op jit(solution)/shard_map/all_to_all | solution.py:58
  355.5 16.8 %all-to-all-start.7 = ((bf16[8,48,4096]{2,1,0:T(8,128)(2,1)}), bf16[8,48,4096]{2,1,0:T(8,128)(2,1)}, u32[]{:S(2)}, u32[]{:S(2)}) async-start(bf16[8,48,4096]{2,1,0:T(8,128)(2,1)} %bitcast.137), calls=%async_computation.7 | async-start | bytes 6291456 | tf_op jit(solution)/shard_map/all_to_all | solution.py:58
  377.6 32.9 %collective-permute-done.1 = bf16[128,4096]{1,0:T(8,128)(2,1)S(1)} collective-permute-done((bf16[128,4096]{1,0:T(8,128)(2,1)S(1)}, bf16[128,4096]{1,0:T(8,128)(2,1)S(1)}, u32[]{:S(2)}, u32[]{:S(2)}) %collective-permute-start.1) | collective-permute-done | bytes 1048608 | tf_op jit(solution)/shard_map/ppermute | solution.py:9
  417.2 6.9 %all-to-all-start.6 = ((bf16[8,48,4096]{2,1,0:T(8,128)(2,1)}), bf16[8,48,4096]{2,1,0:T(8,128)(2,1)S(1)}, u32[]{:S(2)}, u32[]{:S(2)}) async-start(bf16[8,48,4096]{2,1,0:T(8,128)(2,1)} %bitcast.24), calls=%async_computation.6 | async-start | bytes 6291456 | tf_op jit(solution)/shard_map/all_to_all | solution.py:58
  424.2 7.4 %fusion.2 = f32[384,768]{1,0:T(8,128)} fusion(bf16[384,4096]{1,0:T(8,128)(2,1)} %bitcast.28, bf16[1,1,4096,768]{3,2,1,0:T(8,128)(2,1)} %param.13), kind=kOutput, calls=%fused_computation.2 | convolution fusion | flops 2415919104 | bytes 10616832 | tf_op jit(solution)/shard_map/dot_general | solution.py:13
  431.5 30.9 %all-to-all-done.6 = bf16[8,48,4096]{2,1,0:T(8,128)(2,1)S(1)} async-done(((bf16[8,48,4096]{2,1,0:T(8,128)(2,1)}), bf16[8,48,4096]{2,1,0:T(8,128)(2,1)S(1)}, u32[]{:S(2)}, u32[]{:S(2)}) %all-to-all-start.6) | async-done | bytes 3145760 | tf_op jit(solution)/shard_map/all_to_all | solution.py:58
  462.5 6.4 %fusion.24 = f32[384,768]{1,0:T(8,128)} fusion(bf16[384,4096]{1,0:T(8,128)(2,1)S(1)} %bitcast.142, bf16[1,1,768,4096]{3,2,1,0:T(8,128)(2,1)} %param.15), kind=kOutput, calls=%fused_computation.24 | convolution fusion | flops 2415919104 | bytes 10616832 | tf_op jit(solution)/shard_map/dot_general | solution.py:19
  468.9 15.7 %fusion = f32[384,4096]{1,0:T(8,128)} fusion(bf16[1,1,4096,768]{3,2,1,0:T(8,128)(2,1)} %param.13, f32[384,768]{1,0:T(8,128)} %fusion.24, bf16[384,4096]{1,0:T(8,128)(2,1)} %bitcast.28, bf16[1,1,4096,768]{3,2,1,0:T(8,128)(2,1)} %param.14, f32[384,768]{1,0:T(8,128)} %fusion.2), kind=kOutput, calls=%fused_computation | convolution fusion | flops 4834787328 | bytes 24379392 | tf_op jit(solution)/shard_map/dot_general | solution.py:24
  484.6 9.4 %add_convert_fusion = bf16[384,4096]{1,0:T(8,128)(2,1)} fusion(f32[384,4096]{1,0:T(8,128)} %fusion, bf16[1,1,4096,768]{3,2,1,0:T(8,128)(2,1)} %param.14, f32[384,768]{1,0:T(8,128)S(1)} %copy-done.12, f32[384,768]{1,0:T(8,128)S(1)} %copy-done.9), kind=kOutput, calls=%fused_computation.30 | convolution fusion | flops 2420834304 | bytes 18087936 | tf_op jit(solution)/shard_map/dot_general | solution.py:25
  493.9 11.0 %all-to-all-start.8 = ((bf16[8,48,4096]{2,1,0:T(8,128)(2,1)}), bf16[8,48,4096]{2,1,0:T(8,128)(2,1)S(1)}, u32[]{:S(2)}, u32[]{:S(2)}) async-start(bf16[8,48,4096]{2,1,0:T(8,128)(2,1)} %bitcast.138), calls=%async_computation.8 | async-start | bytes 6291456 | tf_op jit(solution)/shard_map/all_to_all | solution.py:58
  505.1 38.1 %all-to-all-done.8 = bf16[8,48,4096]{2,1,0:T(8,128)(2,1)S(1)} async-done(((bf16[8,48,4096]{2,1,0:T(8,128)(2,1)}), bf16[8,48,4096]{2,1,0:T(8,128)(2,1)S(1)}, u32[]{:S(2)}, u32[]{:S(2)}) %all-to-all-start.8) | async-done | bytes 3145760 | tf_op jit(solution)/shard_map/all_to_all | solution.py:58
  546.1 14.9 %collective-permute-done.2 = bf16[128,4096]{1,0:T(8,128)(2,1)S(1)} collective-permute-done((bf16[128,4096]{1,0:T(8,128)(2,1)S(1)}, bf16[128,4096]{1,0:T(8,128)(2,1)S(1)}, u32[]{:S(2)}, u32[]{:S(2)}) %collective-permute-start.2) | collective-permute-done | bytes 1048608 | tf_op jit(solution)/shard_map/ppermute | solution.py:9
  (51 shorter events, 34.1 us)
Async XLA Ops:
  4.8 6.5 %copy-start = (bf16[1,128,4096]{2,1,0:T(8,128)(2,1)S(1)}, bf16[1,128,4096]{2,1,0:T(8,128)(2,1)}, u32[]{:S(2)}) copy-start(bf16[1,128,4096]{2,1,0:T(8,128)(2,1)} %param.8) | copy-start | bytes 3145732
  4.8 44.9 %all-to-all-start.1 = ((bf16[8,48,4096]{2,1,0:T(8,128)(2,1)}), bf16[8,48,4096]{2,1,0:T(8,128)(2,1)}, u32[]{:S(2)}, u32[]{:S(2)}) async-start(bf16[8,48,4096]{2,1,0:T(8,128)(2,1)} %bitcast.7), calls=%async_computation.1 | async-start | bytes 6291456 | tf_op jit(solution)/shard_map/all_to_all | solution.py:58
  49.7 48.9 %all-to-all-start = ((bf16[8,48,4096]{2,1,0:T(8,128)(2,1)}), bf16[8,48,4096]{2,1,0:T(8,128)(2,1)S(1)}, u32[]{:S(2)}, u32[]{:S(2)}) async-start(bf16[8,48,4096]{2,1,0:T(8,128)(2,1)} %bitcast.3), calls=%async_computation | async-start | bytes 6291456 | tf_op jit(solution)/shard_map/all_to_all | solution.py:58
  105.0 15.7 %copy-start.7 = (f32[384,768]{1,0:T(8,128)S(1)}, f32[384,768]{1,0:T(8,128)}, u32[]{:S(2)}) copy-start(f32[384,768]{1,0:T(8,128)} %fusion.10) | copy-start | bytes 3538948
  105.0 15.7 %copy-start.10 = (f32[384,768]{1,0:T(8,128)S(1)}, f32[384,768]{1,0:T(8,128)}, u32[]{:S(2)}) copy-start(f32[384,768]{1,0:T(8,128)} %fusion.28) | copy-start | bytes 3538948
  130.1 43.0 %all-to-all-start.2 = ((bf16[8,48,4096]{2,1,0:T(8,128)(2,1)}), bf16[8,48,4096]{2,1,0:T(8,128)(2,1)S(1)}, u32[]{:S(2)}, u32[]{:S(2)}) async-start(bf16[8,48,4096]{2,1,0:T(8,128)(2,1)} %bitcast.143), calls=%async_computation.2 | async-start | bytes 6291456 | tf_op jit(solution)/shard_map/all_to_all | solution.py:58
  173.0 4.9 copy-start.6
  173.0 57.9 %all-to-all-start.4 = ((bf16[8,48,4096]{2,1,0:T(8,128)(2,1)}), bf16[8,48,4096]{2,1,0:T(8,128)(2,1)}, u32[]{:S(2)}, u32[]{:S(2)}) async-start(bf16[8,48,4096]{2,1,0:T(8,128)(2,1)} %bitcast.136), calls=%async_computation.4 | async-start | bytes 6291456 | tf_op jit(solution)/shard_map/all_to_all | solution.py:58
  177.9 1.2 copy-start.1
  179.9 47.3 %collective-permute-start = (bf16[128,4096]{1,0:T(8,128)(2,1)S(1)}, bf16[128,4096]{1,0:T(8,128)(2,1)S(1)}, u32[]{:S(2)}, u32[]{:S(2)}) collective-permute-start(bf16[128,4096]{1,0:T(8,128)(2,1)S(1)} %fusion.37), channel_id=1, source_target_pairs={{0,120},{8,0},{16,8},{24,16},{32,24},{40,32},{48,40},{56,48},{64,5... | collective-permute-start | bytes 3145736 | tf_op jit(solution)/shard_map/ppermute | solution.py:9
  227.2 1.0 copy-start.2
  230.9 42.9 %all-to-all-start.3 = ((bf16[8,48,4096]{2,1,0:T(8,128)(2,1)}), bf16[8,48,4096]{2,1,0:T(8,128)(2,1)S(1)}, u32[]{:S(2)}, u32[]{:S(2)}) async-start(bf16[8,48,4096]{2,1,0:T(8,128)(2,1)} %bitcast.15), calls=%async_computation.3 | async-start | bytes 6291456 | tf_op jit(solution)/shard_map/all_to_all | solution.py:58
  280.2 15.7 %copy-start.8 = (f32[384,768]{1,0:T(8,128)S(1)}, f32[384,768]{1,0:T(8,128)}, u32[]{:S(2)}) copy-start(f32[384,768]{1,0:T(8,128)} %fusion.6) | copy-start | bytes 3538948
  280.2 15.7 %copy-start.11 = (f32[384,768]{1,0:T(8,128)S(1)}, f32[384,768]{1,0:T(8,128)}, u32[]{:S(2)}) copy-start(f32[384,768]{1,0:T(8,128)} %fusion.26) | copy-start | bytes 3538948
  305.3 50.3 %all-to-all-start.5 = ((bf16[8,48,4096]{2,1,0:T(8,128)(2,1)}), bf16[8,48,4096]{2,1,0:T(8,128)(2,1)S(1)}, u32[]{:S(2)}, u32[]{:S(2)}) async-start(bf16[8,48,4096]{2,1,0:T(8,128)(2,1)} %bitcast.141), calls=%async_computation.5 | async-start | bytes 6291456 | tf_op jit(solution)/shard_map/all_to_all | solution.py:58
  355.5 61.7 %all-to-all-start.7 = ((bf16[8,48,4096]{2,1,0:T(8,128)(2,1)}), bf16[8,48,4096]{2,1,0:T(8,128)(2,1)}, u32[]{:S(2)}, u32[]{:S(2)}) async-start(bf16[8,48,4096]{2,1,0:T(8,128)(2,1)} %bitcast.137), calls=%async_computation.7 | async-start | bytes 6291456 | tf_op jit(solution)/shard_map/all_to_all | solution.py:58
  372.4 1.2 copy-start.3
  374.4 36.1 %collective-permute-start.1 = (bf16[128,4096]{1,0:T(8,128)(2,1)S(1)}, bf16[128,4096]{1,0:T(8,128)(2,1)S(1)}, u32[]{:S(2)}, u32[]{:S(2)}) collective-permute-start(bf16[128,4096]{1,0:T(8,128)(2,1)S(1)} %add_convert_fusion.4), channel_id=1, source_target_pairs={{0,120},{8,0},{16,8},{24,16},{32,24},{40,32},{48,40},{56,48},{64,5... | collective-permute-start | bytes 3145736 | tf_op jit(solution)/shard_map/ppermute | solution.py:9
  410.5 1.0 copy-start.4
  417.2 45.2 %all-to-all-start.6 = ((bf16[8,48,4096]{2,1,0:T(8,128)(2,1)}), bf16[8,48,4096]{2,1,0:T(8,128)(2,1)S(1)}, u32[]{:S(2)}, u32[]{:S(2)}) async-start(bf16[8,48,4096]{2,1,0:T(8,128)(2,1)} %bitcast.24), calls=%async_computation.6 | async-start | bytes 6291456 | tf_op jit(solution)/shard_map/all_to_all | solution.py:58
  468.9 15.7 %copy-start.9 = (f32[384,768]{1,0:T(8,128)S(1)}, f32[384,768]{1,0:T(8,128)}, u32[]{:S(2)}) copy-start(f32[384,768]{1,0:T(8,128)} %fusion.2) | copy-start | bytes 3538948
  468.9 15.7 %copy-start.12 = (f32[384,768]{1,0:T(8,128)S(1)}, f32[384,768]{1,0:T(8,128)}, u32[]{:S(2)}) copy-start(f32[384,768]{1,0:T(8,128)} %fusion.24) | copy-start | bytes 3538948
  493.9 49.3 %all-to-all-start.8 = ((bf16[8,48,4096]{2,1,0:T(8,128)(2,1)}), bf16[8,48,4096]{2,1,0:T(8,128)(2,1)S(1)}, u32[]{:S(2)}, u32[]{:S(2)}) async-start(bf16[8,48,4096]{2,1,0:T(8,128)(2,1)} %bitcast.138), calls=%async_computation.8 | async-start | bytes 6291456 | tf_op jit(solution)/shard_map/all_to_all | solution.py:58
  543.2 1.2 copy-start.5
  545.2 15.8 %collective-permute-start.2 = (bf16[128,4096]{1,0:T(8,128)(2,1)S(1)}, bf16[128,4096]{1,0:T(8,128)(2,1)S(1)}, u32[]{:S(2)}, u32[]{:S(2)}) collective-permute-start(bf16[128,4096]{1,0:T(8,128)(2,1)S(1)} %add_convert_fusion.3), channel_id=1, source_target_pairs={{0,120},{8,0},{16,8},{24,16},{32,24},{40,32},{48,40},{56,48},{64,5... | collective-permute-start | bytes 3145736 | tf_op jit(solution)/shard_map/ppermute | solution.py:9

commit v2 on v1

v2 whole, which is shorter than its diff:
```python
import jax
import jax.numpy as jnp
from jax import lax
from jax.sharding import PartitionSpec as P


def shifted(x, axis, by):
    devices = lax.axis_size(axis)
    return lax.ppermute(x, axis, [(i, (i + by) % devices) for i in range(devices)])


def forward_part(input_part, gate_proj, up_proj):
    pre_gate = jnp.einsum("scjl,jlh->sch", input_part, gate_proj, preferred_element_type=jnp.float32)
    pre_up = jnp.einsum("scjl,jlh->sch", input_part, up_proj, preferred_element_type=jnp.float32)
    return pre_gate, pre_up


def backward_part(grad_part, pre_gate, pre_up, gate_proj, up_proj, down_proj):
    grad_hidden = jnp.einsum("scjl,hjl->sch", grad_part, down_proj, preferred_element_type=jnp.float32)
    sigma = jax.nn.sigmoid(pre_gate)
    derivative = sigma * (1.0 + pre_gate * (1.0 - sigma))
    grad_gate = (grad_hidden * pre_up * derivative).astype(jnp.bfloat16)
    grad_up = (grad_hidden * pre_gate * sigma).astype(jnp.bfloat16)
    summed = jnp.einsum("sch,jlh->scjl", grad_gate, gate_proj, preferred_element_type=jnp.float32)
    summed = summed + jnp.einsum("sch,jlh->scjl", grad_up, up_proj, preferred_element_type=jnp.float32)
    return summed.astype(jnp.bfloat16)


def per_device(grad_in, saved_inputs, expert_ids, slots, gates, w_gate, w_up, w_down):
    groups = lax.axis_size("expert")
    rows_dev = grad_in.shape[1]
    width = grad_in.shape[2]
    rounds = saved_inputs.shape[0]
    capacity = 9 * rows_dev * expert_ids.shape[-1] // (8 * groups)
    lanes = 128
    pieces = width // lanes
    columns = groups * capacity
    hidden = w_gate.shape[-1]
    gate_proj = w_gate[0, 0].reshape(pieces, lanes, hidden)
    up_proj = w_up[0, 0].reshape(pieces, lanes, hidden)
    down_proj = w_down[0, 0].reshape(hidden, pieces, lanes)
    column_ids = jnp.arange(columns, dtype=jnp.int32)

    def route_plan(step):
        route_ids = expert_ids[step, 0]
        slot_ids = slots[step, 0]
        target = jnp.where(slot_ids < capacity, route_ids * capacity + slot_ids, -1)
        hit = target[:, :, None] == column_ids[None, None, :]
        dispatch = jnp.any(hit, axis=1).T.astype(jnp.bfloat16).reshape(groups, capacity, rows_dev)
        weights = jnp.sum(jnp.where(hit, gates[step, 0][:, :, None], 0.0), axis=1)
        weights_hi = weights.astype(jnp.bfloat16)
        weights_lo = (weights - weights_hi.astype(jnp.float32)).astype(jnp.bfloat16)
        shape = (rows_dev, groups, capacity)
        return dispatch, weights_hi.reshape(shape), weights_lo.reshape(shape)

    def collect(dispatch, rows):
        picked = jnp.einsum("ect,tjl->ecjl", dispatch, rows, preferred_element_type=jnp.float32)
        return picked.astype(jnp.bfloat16)

    def exchange(buffer):
        flat = buffer.reshape(groups, capacity * pieces, lanes)
        moved = lax.all_to_all(flat, "expert", split_axis=0, concat_axis=0, tiled=True)
        return moved.reshape(groups, capacity, pieces, lanes)

    plans = [route_plan(step) for step in range(rounds)]
    forwards = []
    for step in range(rounds):
        rows = saved_inputs[step, 0].reshape(rows_dev, pieces, lanes)
        input_part = exchange(collect(plans[step][0], rows))
        forwards.append(forward_part(input_part, gate_proj, up_proj))

    present_block = grad_in[0].reshape(rows_dev, pieces, lanes)
    for step in range(rounds):
        dispatch, weights_hi, weights_lo = plans[step]
        grad_part = exchange(collect(dispatch, present_block))
        pre_gate, pre_up = forwards[step]
        result = backward_part(grad_part, pre_gate, pre_up, gate_proj, up_proj, down_proj)
        arrived = exchange(result)
        combined = jnp.einsum("tec,ecjl->tjl", weights_hi, arrived, preferred_element_type=jnp.float32)
        combined = combined + jnp.einsum("tec,ecjl->tjl", weights_lo, arrived, preferred_element_type=jnp.float32)
        summed = present_block.astype(jnp.float32) + combined
        present_block = shifted(summed.astype(jnp.bfloat16), "section", -1)
    return present_block.reshape(1, rows_dev, width)


def solution(mesh):
    placed = (
        P("section", "expert", None),
        P(None, "section", "expert", None),
        P(None, "section", "expert", None),
        P(None, "section", "expert", None),
        P(None, "section", "expert", None),
        P("section", "expert", None, None),
        P("section", "expert", None, None),
        P("section", "expert", None, None),
    )
    return jax.shard_map(
        per_device,
        mesh=mesh,
        in_specs=placed,
        out_specs=P("section", "expert", None),
        check_vma=False,
    )
```

time: 573 us -> 479 us (0.84)
  waiting for transfers between devices: 332 us -> 246 us
  local copies, waits for them, and re-layouts: 4.14 us -> 43.3 us
  starting transfers between devices: 82.9 us -> 60.6 us
  matrix products: 141 us -> 119 us
    all_to_all x9, waiting for transfers between devices: 238 us -> 160 us  [exchange(): lax.all_to_all(flat, 'expert', split_axis=0, concat_axis=0, tiled=True)]
    dot_general x24, matrix products: 141 us -> 119 us  [the longest x3 41.2 us: backward_part(): jnp.einsum('sch,jlh->scjl', grad_gate, gate_proj, preferred_element_type=...]
    all_to_all x9, starting transfers between devices: 77.9 us -> 56.1 us  [exchange(): lax.all_to_all(flat, 'expert', split_axis=0, concat_axis=0, tiled=True)]
    convert_element_type x0 -> x9, local copies, waits for them, and re-layouts: none -> 17.4 us  [the longest x6 11.6 us: collect(): return picked.astype(jnp.bfloat16)]
    unnamed x27 -> x41, local copies, waits for them, and re-layouts: 4.14 us -> 16.4 us
    ppermute x3, waiting for transfers between devices: 94.2 us -> 85.2 us  [shifted(): lax.ppermute(x, axis, [(i, (i + by) % devices) for i in range(devices)])]
  transfers between devices with their start and end apart: 12 -> 12, of which waited for: 11 -> 10; matrix products, arithmetic and copies ran while one was open for 7% -> 11% of each run, Pallas kernels for 0% -> 0%
where the time goes in v2:
time: 479 us; the launch traced here: 472 us
  waiting for transfers between devices  246 us (51%)
  matrix products  119 us (25%)
  starting transfers between devices  60.6 us (13%)
  local copies, waits for them, and re-layouts  43.3 us (9%)
    all_to_all x9, waiting for transfers between devices, exchange(): lax.all_to_all(flat, 'expert', split_axis=0, concat_axis=0, tiled=True)  160 us
    ppermute x3, waiting for transfers between devices, shifted(): lax.ppermute(x, axis, [(i, (i + by) % devices) for i in range(devices)])  85.2 us
    all_to_all x9, starting transfers between devices, exchange(): lax.all_to_all(flat, 'expert', split_axis=0, concat_axis=0, tiled=True)  56.1 us
    dot_general x3, matrix products, backward_part(): jnp.einsum('sch,jlh->scjl', grad_gate, gate_proj, preferred_element_type=...  41.2 us
    dot_general x3, matrix products, backward_part(): jnp.einsum('scjl,hjl->sch', grad_part, down_proj, preferred_element_type=...  24.4 us
    dot_general x3, matrix products, backward_part(): jnp.einsum('sch,jlh->scjl', grad_up, up_proj, preferred_element_type=jnp....  23.6 us
    dot_general x3, matrix products, forward_part(): jnp.einsum('scjl,jlh->sch', input_part, gate_proj, preferred_element_type...  16.6 us
    unnamed x41, local copies, waits for them, and re-layouts  16.4 us
  transfers between devices with their start and end apart: 12, of which 10 were waited for; matrix products, arithmetic and copies ran while one was open for 11% of the time, Pallas kernels for 0%

profile of v2, /device:TPU:1, one launch (start us, length us, event | category | flops | bytes accessed | tf_op | source)
XLA Modules:
  0.0 472.2 jit_solution(5501906605207671221)
XLA Ops:
  8.9 6.4 %all-to-all-start.1 = ((bf16[8,1152,128]{2,1,0:T(8,128)(2,1)}), bf16[8,1152,128]{2,1,0:T(8,128)(2,1)S(1)}, u32[]{:S(2)}, u32[]{:S(2)}) async-start(bf16[8,1152,128]{2,1,0:T(8,128)(2,1)} %bitcast.282), calls=%async_computation.1 | async-start | bytes 4718592 | tf_op jit(solution)/shard_map/all_to_all | solution.py:62
  19.6 25.5 %all-to-all-done.1 = bf16[8,1152,128]{2,1,0:T(8,128)(2,1)S(1)} async-done(((bf16[8,1152,128]{2,1,0:T(8,128)(2,1)}), bf16[8,1152,128]{2,1,0:T(8,128)(2,1)S(1)}, u32[]{:S(2)}, u32[]{:S(2)}) %all-to-all-start.1) | async-done | bytes 2359328 | tf_op jit(solution)/shard_map/all_to_all | solution.py:62
  46.6 6.4 %all-to-all-start = ((bf16[8,1152,128]{2,1,0:T(8,128)(2,1)}), bf16[8,1152,128]{2,1,0:T(8,128)(2,1)}, u32[]{:S(2)}, u32[]{:S(2)}) async-start(bf16[8,1152,128]{2,1,0:T(8,128)(2,1)} %bitcast.280), calls=%async_computation | async-start | bytes 4718592 | tf_op jit(solution)/shard_map/all_to_all | solution.py:62
  53.0 7.6 %copy.132 = bf16[96,8,32,128]{3,2,1,0:T(8,128)(2,1)} copy(bf16[96,8,32,128]{3,1,2,0:T(8,128)(2,1)} %bitcast.283) | data formatting | bytes 12582912
  60.6 3.7 fusion.51
  64.3 18.5 %all-to-all-done = bf16[8,1152,128]{2,1,0:T(8,128)(2,1)} async-done(((bf16[8,1152,128]{2,1,0:T(8,128)(2,1)}), bf16[8,1152,128]{2,1,0:T(8,128)(2,1)}, u32[]{:S(2)}, u32[]{:S(2)}) %all-to-all-start) | async-done | bytes 2359328 | tf_op jit(solution)/shard_map/all_to_all | solution.py:62
  82.7 8.7 %fusion.66 = f32[8,36,768]{2,1,0:T(8,128)} fusion(bf16[768,32,128]{2,1,0:T(8,128)(2,1)} %bitcast.284, bf16[8,36,32,128]{3,2,1,0:T(8,128)(2,1)} %bitcast.8), kind=kOutput, calls=%fused_computation.60 | convolution fusion | flops 1811939328 | bytes 9535488 | tf_op jit(solution)/shard_map/scjl,hjl->sch/dot_general | solution.py:19
  91.5 13.3 %fusion.129 = f32[8,36,32,128]{3,1,2,0:T(8,128)} fusion(bf16[32,128,768,1]{2,1,0,3:T(8,128)(2,1)} %bitcast.258, f32[8,36,768]{2,1,0:T(8,128)} %fusion.66, bf16[32,128,768,1]{2,1,0,3:T(8,128)(2,1)} %bitcast.252, bf16[8,36,32,128]{3,2,1,0:T(8,128)(2,1)S(1)} %bitcast.273, f32[8,36,768]{2,1,0:T(8,128)} %fusion.51), kind=kOutput, calls=%fused_computation.88 | convolution fusion | flops 3626090496 | bytes 21430272 | tf_op jit(solution)/shard_map/sch,jlh->scjl/dot_general | solution.py:24
  104.8 7.4 %add_convert_fusion.2 = bf16[8,36,32,128]{3,1,2,0:T(8,128)(2,1)S(1)} fusion(f32[8,36,32,128]{3,1,2,0:T(8,128)} %fusion.129, bf16[32,128,768,1]{2,1,0,3:T(8,128)(2,1)} %bitcast.253, f32[8,36,768]{2,1,0:T(8,128)} %fusion.66, f32[8,36,768]{2,1,0:T(8,128)} %fusion.51), kind=kOutput, calls=%fused_computation.8 | convolution fusion | flops 1815625728 | bytes 15138816 | tf_op jit(solution)/shard_map/sch,jlh->scjl/dot_general | solution.py:25
  114.1 3.7 all-to-all-start.2
  126.4 21.3 %all-to-all-done.2 = bf16[8,1152,128]{2,1,0:T(8,128)(2,1)S(1)} async-done(((bf16[8,1152,128]{2,1,0:T(8,128)(2,1)}), bf16[8,1152,128]{2,1,0:T(8,128)(2,1)S(1)}, u32[]{:S(2)}, u32[]{:S(2)}) %all-to-all-start.2) | async-done | bytes 2359328 | tf_op jit(solution)/shard_map/all_to_all | solution.py:62
  147.7 6.6 %all-to-all-start.4 = ((bf16[8,1152,128]{2,1,0:T(8,128)(2,1)}), bf16[8,1152,128]{2,1,0:T(8,128)(2,1)}, u32[]{:S(2)}, u32[]{:S(2)}) async-start(bf16[8,1152,128]{2,1,0:T(8,128)(2,1)} %bitcast.277), calls=%async_computation.4 | async-start | bytes 4718592 | tf_op jit(solution)/shard_map/all_to_all | solution.py:62
  158.9 36.5 %collective-permute-done = bf16[128,32,128]{2,0,1:T(8,128)(2,1)S(1)} collective-permute-done((bf16[128,32,128]{2,0,1:T(8,128)(2,1)S(1)}, bf16[128,32,128]{2,0,1:T(8,128)(2,1)S(1)}, u32[]{:S(2)}, u32[]{:S(2)}) %collective-permute-start) | collective-permute-done | bytes 1048608 | tf_op jit(solution)/shard_map/ppermute | solution.py:9
  199.1 5.0 %all-to-all-start.3 = ((bf16[8,1152,128]{2,1,0:T(8,128)(2,1)}), bf16[8,1152,128]{2,1,0:T(8,128)(2,1)S(1)}, u32[]{:S(2)}, u32[]{:S(2)}) async-start(bf16[8,1152,128]{2,1,0:T(8,128)(2,1)} %bitcast.42), calls=%async_computation.3 | async-start | bytes 4718592 | tf_op jit(solution)/shard_map/all_to_all | solution.py:62
  204.2 5.8 %fusion.57 = f32[8,36,768]{2,1,0:T(8,128)S(1)} fusion(bf16[32,128,768,1]{2,1,0,3:T(8,128)(2,1)} %bitcast.259, bf16[8,36,32,128]{3,2,1,0:T(8,128)(2,1)} %bitcast.50), kind=kOutput, calls=%fused_computation.57 | convolution fusion | flops 1811939328 | bytes 9535488 | tf_op jit(solution)/shard_map/scjl,jlh->sch/dot_general | solution.py:13
  210.0 19.4 %all-to-all-done.3 = bf16[8,1152,128]{2,1,0:T(8,128)(2,1)S(1)} async-done(((bf16[8,1152,128]{2,1,0:T(8,128)(2,1)}), bf16[8,1152,128]{2,1,0:T(8,128)(2,1)S(1)}, u32[]{:S(2)}, u32[]{:S(2)}) %all-to-all-start.3) | async-done | bytes 2359328 | tf_op jit(solution)/shard_map/all_to_all | solution.py:62
  229.5 7.8 %fusion.71 = f32[8,36,768]{2,1,0:T(8,128)} fusion(bf16[768,32,128]{2,1,0:T(8,128)(2,1)} %bitcast.285, bf16[8,36,32,128]{3,2,1,0:T(8,128)(2,1)S(1)} %bitcast.292), kind=kOutput, calls=%fused_computation.61 | convolution fusion | flops 1811939328 | bytes 9535488 | tf_op jit(solution)/shard_map/scjl,hjl->sch/dot_general | solution.py:19
  237.3 13.8 %fusion.126 = f32[8,36,32,128]{3,1,2,0:T(8,128)} fusion(bf16[32,128,768,1]{2,1,0,3:T(8,128)(2,1)} %bitcast.260, f32[8,36,768]{2,1,0:T(8,128)} %fusion.71, bf16[32,128,768,1]{2,1,0,3:T(8,128)(2,1)} %bitcast.254, bf16[8,36,32,128]{3,2,1,0:T(8,128)(2,1)} %bitcast.50, f32[8,36,768]{2,1,0:T(8,128)S(1)} %fusion.57), kind=kOutput, calls=%fused_computation.87 | convolution fusion | flops 3626090496 | bytes 21430272 | tf_op jit(solution)/shard_map/sch,jlh->scjl/dot_general | solution.py:24
  251.1 8.0 %add_convert_fusion.1 = bf16[8,36,32,128]{3,1,2,0:T(8,128)(2,1)S(1)} fusion(f32[8,36,32,128]{3,1,2,0:T(8,128)} %fusion.126, bf16[32,128,768,1]{2,1,0,3:T(8,128)(2,1)} %bitcast.255, f32[8,36,768]{2,1,0:T(8,128)S(1)} %copy-done.11, f32[8,36,768]{2,1,0:T(8,128)S(1)} %fusion.57), kind=kOutput, calls=%fused_computation.7 | convolution fusion | flops 1815625728 | bytes 15138816 | tf_op jit(solution)/shard_map/sch,jlh->scjl/dot_general | solution.py:25
  261.0 3.9 all-to-all-start.5
  270.1 24.8 %all-to-all-done.5 = bf16[8,1152,128]{2,1,0:T(8,128)(2,1)S(1)} async-done(((bf16[8,1152,128]{2,1,0:T(8,128)(2,1)}), bf16[8,1152,128]{2,1,0:T(8,128)(2,1)S(1)}, u32[]{:S(2)}, u32[]{:S(2)}) %all-to-all-start.5) | async-done | bytes 2359328 | tf_op jit(solution)/shard_map/all_to_all | solution.py:62
  294.9 9.3 %all-to-all-start.7 = ((bf16[8,1152,128]{2,1,0:T(8,128)(2,1)}), bf16[8,1152,128]{2,1,0:T(8,128)(2,1)}, u32[]{:S(2)}, u32[]{:S(2)}) async-start(bf16[8,1152,128]{2,1,0:T(8,128)(2,1)} %bitcast.278), calls=%async_computation.7 | async-start | bytes 4718592 | tf_op jit(solution)/shard_map/all_to_all | solution.py:62
  308.1 33.8 %collective-permute-done.1 = bf16[128,32,128]{2,0,1:T(8,128)(2,1)S(1)} collective-permute-done((bf16[128,32,128]{2,0,1:T(8,128)(2,1)S(1)}, bf16[128,32,128]{2,0,1:T(8,128)(2,1)S(1)}, u32[]{:S(2)}, u32[]{:S(2)}) %collective-permute-start.1) | collective-permute-done | bytes 1048608 | tf_op jit(solution)/shard_map/ppermute | solution.py:9
  344.7 4.6 all-to-all-start.6
  349.3 7.1 %fusion.63 = f32[8,36,768]{2,1,0:T(8,128)} fusion(bf16[32,128,768,1]{2,1,0,3:T(8,128)(2,1)} %bitcast.261, bf16[8,36,32,128]{3,2,1,0:T(8,128)(2,1)} %bitcast.81), kind=kOutput, calls=%fused_computation.59 | convolution fusion | flops 1811939328 | bytes 9535488 | tf_op jit(solution)/shard_map/scjl,jlh->sch/dot_general | solution.py:13
  356.4 22.4 %all-to-all-done.6 = bf16[8,1152,128]{2,1,0:T(8,128)(2,1)S(1)} async-done(((bf16[8,1152,128]{2,1,0:T(8,128)(2,1)}), bf16[8,1152,128]{2,1,0:T(8,128)(2,1)S(1)}, u32[]{:S(2)}, u32[]{:S(2)}) %all-to-all-start.6) | async-done | bytes 2359328 | tf_op jit(solution)/shard_map/all_to_all | solution.py:62
  378.9 7.8 %fusion.76 = f32[8,36,768]{2,1,0:T(8,128)} fusion(bf16[768,32,128]{2,1,0:T(8,128)(2,1)} %bitcast.286, bf16[8,36,32,128]{3,2,1,0:T(8,128)(2,1)S(1)} %bitcast.291), kind=kOutput, calls=%fused_computation.62 | convolution fusion | flops 1811939328 | bytes 9535488 | tf_op jit(solution)/shard_map/scjl,hjl->sch/dot_general | solution.py:19
  386.7 14.1 %fusion.123 = f32[8,36,32,128]{3,1,2,0:T(8,128)} fusion(bf16[32,128,768,1]{2,1,0,3:T(8,128)(2,1)} %bitcast.262, f32[8,36,768]{2,1,0:T(8,128)} %fusion.76, bf16[32,128,768,1]{2,1,0,3:T(8,128)(2,1)} %bitcast.256, bf16[8,36,32,128]{3,2,1,0:T(8,128)(2,1)} %bitcast.81, f32[8,36,768]{2,1,0:T(8,128)} %fusion.63), kind=kOutput, calls=%fused_computation.86 | convolution fusion | flops 3626090496 | bytes 21430272 | tf_op jit(solution)/shard_map/sch,jlh->scjl/dot_general | solution.py:24
  400.8 8.2 %add_convert_fusion = bf16[8,36,32,128]{3,1,2,0:T(8,128)(2,1)S(1)} fusion(f32[8,36,32,128]{3,1,2,0:T(8,128)} %fusion.123, bf16[32,128,768,1]{2,1,0,3:T(8,128)(2,1)} %bitcast.257, f32[8,36,768]{2,1,0:T(8,128)S(1)} %copy-done.10, f32[8,36,768]{2,1,0:T(8,128)S(1)} %copy-done.9), kind=kOutput, calls=%fused_computation.6 | convolution fusion | flops 1815625728 | bytes 15138816 | tf_op jit(solution)/shard_map/sch,jlh->scjl/dot_general | solution.py:25
  410.9 10.0 %all-to-all-start.8 = ((bf16[8,1152,128]{2,1,0:T(8,128)(2,1)}), bf16[8,1152,128]{2,1,0:T(8,128)(2,1)S(1)}, u32[]{:S(2)}, u32[]{:S(2)}) async-start(bf16[8,1152,128]{2,1,0:T(8,128)(2,1)} %bitcast.281), calls=%async_computation.8 | async-start | bytes 4718592 | tf_op jit(solution)/shard_map/all_to_all | solution.py:62
  422.4 28.5 %all-to-all-done.8 = bf16[8,1152,128]{2,1,0:T(8,128)(2,1)S(1)} async-done(((bf16[8,1152,128]{2,1,0:T(8,128)(2,1)}), bf16[8,1152,128]{2,1,0:T(8,128)(2,1)S(1)}, u32[]{:S(2)}, u32[]{:S(2)}) %all-to-all-start.8) | async-done | bytes 2359328 | tf_op jit(solution)/shard_map/all_to_all | solution.py:62
  455.1 14.9 %collective-permute-done.2 = bf16[128,32,128]{2,0,1:T(8,128)(2,1)S(1)} collective-permute-done((bf16[128,32,128]{2,0,1:T(8,128)(2,1)S(1)}, bf16[128,32,128]{2,0,1:T(8,128)(2,1)S(1)}, u32[]{:S(2)}, u32[]{:S(2)}) %collective-permute-start.2) | collective-permute-done | bytes 1048608 | tf_op jit(solution)/shard_map/ppermute | solution.py:9
  (84 shorter events, 56.5 us)
Async XLA Ops:
  1.3 0.6 copy-start.13
  8.9 36.2 %all-to-all-start.1 = ((bf16[8,1152,128]{2,1,0:T(8,128)(2,1)}), bf16[8,1152,128]{2,1,0:T(8,128)(2,1)S(1)}, u32[]{:S(2)}, u32[]{:S(2)}) async-start(bf16[8,1152,128]{2,1,0:T(8,128)(2,1)} %bitcast.282), calls=%async_computation.1 | async-start | bytes 4718592 | tf_op jit(solution)/shard_map/all_to_all | solution.py:62
  45.1 1.5 copy-start
  46.6 14.0 %slice-start = ((s8[6291456]{0:T(1024)(128)(4,1)}), s8[2097152]{0:T(1024)(128)(4,1)S(1)}, s32[]{:S(2)}) async-start(s8[6291456]{0:T(1024)(128)(4,1)} %bitcast.263), calls=%async_computation.9 | async-start | bytes 4194304
  46.6 36.2 %all-to-all-start = ((bf16[8,1152,128]{2,1,0:T(8,128)(2,1)}), bf16[8,1152,128]{2,1,0:T(8,128)(2,1)}, u32[]{:S(2)}, u32[]{:S(2)}) async-start(bf16[8,1152,128]{2,1,0:T(8,128)(2,1)} %bitcast.280), calls=%async_computation | async-start | bytes 4718592 | tf_op jit(solution)/shard_map/all_to_all | solution.py:62
  52.9 7.7 %slice-start.1 = ((s8[6291456]{0:T(1024)(128)(4,1)}), s8[4194304]{0:T(1024)(128)(4,1)S(1)}, s32[]{:S(2)}) async-start(s8[6291456]{0:T(1024)(128)(4,1)} %bitcast.263), calls=%async_computation.10 | async-start | bytes 8388608
  53.0 7.7 %copy-start.1 = (bf16[8,1152,128]{2,1,0:T(8,128)(2,1)S(1)}, bf16[8,1152,128]{2,1,0:T(8,128)(2,1)}, u32[]{:S(2)}) copy-start(bf16[8,1152,128]{2,1,0:T(8,128)(2,1)} %copy-done) | copy-start | bytes 7077892
  82.7 8.7 %copy-start.2 = (bf16[8,1152,128]{2,1,0:T(8,128)(2,1)S(1)}, bf16[8,1152,128]{2,1,0:T(8,128)(2,1)}, u32[]{:S(2)}) copy-start(bf16[8,1152,128]{2,1,0:T(8,128)(2,1)} %copy-done) | copy-start | bytes 7077892
  114.1 3.8 copy-start.15
  114.1 33.6 %all-to-all-start.2 = ((bf16[8,1152,128]{2,1,0:T(8,128)(2,1)}), bf16[8,1152,128]{2,1,0:T(8,128)(2,1)S(1)}, u32[]{:S(2)}, u32[]{:S(2)}) async-start(bf16[8,1152,128]{2,1,0:T(8,128)(2,1)} %bitcast.276), calls=%async_computation.2 | async-start | bytes 4718592 | tf_op jit(solution)/shard_map/all_to_all | solution.py:62
  126.4 28.0 %copy-start.6 = (f32[128,8,36]{0,2,1:T(8,128)S(1)}, f32[128,8,36]{0,2,1:T(8,128)}, u32[]{:S(2)}) copy-start(f32[128,8,36]{0,2,1:T(8,128)} %reduce_sum.34) | copy-start | bytes 442372
  147.7 51.4 %all-to-all-start.4 = ((bf16[8,1152,128]{2,1,0:T(8,128)(2,1)}), bf16[8,1152,128]{2,1,0:T(8,128)(2,1)}, u32[]{:S(2)}, u32[]{:S(2)}) async-start(bf16[8,1152,128]{2,1,0:T(8,128)(2,1)} %bitcast.277), calls=%async_computation.4 | async-start | bytes 4718592 | tf_op jit(solution)/shard_map/all_to_all | solution.py:62
  154.3 1.2 copy-start.5
  156.7 38.6 %collective-permute-start = (bf16[128,32,128]{2,0,1:T(8,128)(2,1)S(1)}, bf16[128,32,128]{2,0,1:T(8,128)(2,1)S(1)}, u32[]{:S(2)}, u32[]{:S(2)}) collective-permute-start(bf16[128,32,128]{2,0,1:T(8,128)(2,1)S(1)} %fusion.41), channel_id=1, source_target_pairs={{0,120},{8,0},{16,8},{24,16},{32,24},{40,32},{48,40},{56,48},{64,5... | collective-permute-start | bytes 3145736 | tf_op jit(solution)/shard_map/ppermute | solution.py:9
  195.4 1.0 copy-start.3
  199.1 30.3 %all-to-all-start.3 = ((bf16[8,1152,128]{2,1,0:T(8,128)(2,1)}), bf16[8,1152,128]{2,1,0:T(8,128)(2,1)S(1)}, u32[]{:S(2)}, u32[]{:S(2)}) async-start(bf16[8,1152,128]{2,1,0:T(8,128)(2,1)} %bitcast.42), calls=%async_computation.3 | async-start | bytes 4718592 | tf_op jit(solution)/shard_map/all_to_all | solution.py:62
  237.3 13.8 %copy-start.11 = (f32[8,36,768]{2,1,0:T(8,128)S(1)}, f32[8,36,768]{2,1,0:T(8,128)}, u32[]{:S(2)}) copy-start(f32[8,36,768]{2,1,0:T(8,128)} %fusion.71) | copy-start | bytes 2654212
  261.0 3.9 copy-start.12
  261.0 3.9 copy-start.14
  261.0 33.9 %all-to-all-start.5 = ((bf16[8,1152,128]{2,1,0:T(8,128)(2,1)}), bf16[8,1152,128]{2,1,0:T(8,128)(2,1)S(1)}, u32[]{:S(2)}, u32[]{:S(2)}) async-start(bf16[8,1152,128]{2,1,0:T(8,128)(2,1)} %bitcast.279), calls=%async_computation.5 | async-start | bytes 4718592 | tf_op jit(solution)/shard_map/all_to_all | solution.py:62
  270.1 34.1 %copy-start.7 = (f32[128,8,36]{0,2,1:T(8,128)S(1)}, f32[128,8,36]{0,2,1:T(8,128)}, u32[]{:S(2)}) copy-start(f32[128,8,36]{0,2,1:T(8,128)} %reduce_sum.36) | copy-start | bytes 442372
  294.9 49.8 %all-to-all-start.7 = ((bf16[8,1152,128]{2,1,0:T(8,128)(2,1)}), bf16[8,1152,128]{2,1,0:T(8,128)(2,1)}, u32[]{:S(2)}, u32[]{:S(2)}) async-start(bf16[8,1152,128]{2,1,0:T(8,128)(2,1)} %bitcast.278), calls=%async_computation.7 | async-start | bytes 4718592 | tf_op jit(solution)/shard_map/all_to_all | solution.py:62
  304.2 1.2 copy-start.4
  306.6 35.3 %collective-permute-start.1 = (bf16[128,32,128]{2,0,1:T(8,128)(2,1)S(1)}, bf16[128,32,128]{2,0,1:T(8,128)(2,1)S(1)}, u32[]{:S(2)}, u32[]{:S(2)}) collective-permute-start(bf16[128,32,128]{2,0,1:T(8,128)(2,1)S(1)} %fusion.39), channel_id=1, source_target_pairs={{0,120},{8,0},{16,8},{24,16},{32,24},{40,32},{48,40},{56,48},{64,5... | collective-permute-start | bytes 3145736 | tf_op jit(solution)/shard_map/ppermute | solution.py:9
  344.7 34.2 %all-to-all-start.6 = ((bf16[8,1152,128]{2,1,0:T(8,128)(2,1)}), bf16[8,1152,128]{2,1,0:T(8,128)(2,1)S(1)}, u32[]{:S(2)}, u32[]{:S(2)}) async-start(bf16[8,1152,128]{2,1,0:T(8,128)(2,1)} %bitcast.73), calls=%async_computation.6 | async-start | bytes 4718592 | tf_op jit(solution)/shard_map/all_to_all | solution.py:62
  386.7 14.1 %copy-start.9 = (f32[8,36,768]{2,1,0:T(8,128)S(1)}, f32[8,36,768]{2,1,0:T(8,128)}, u32[]{:S(2)}) copy-start(f32[8,36,768]{2,1,0:T(8,128)} %fusion.63) | copy-start | bytes 2654212
  386.7 14.1 %copy-start.10 = (f32[8,36,768]{2,1,0:T(8,128)S(1)}, f32[8,36,768]{2,1,0:T(8,128)}, u32[]{:S(2)}) copy-start(f32[8,36,768]{2,1,0:T(8,128)} %fusion.76) | copy-start | bytes 2654212
  410.9 39.9 %all-to-all-start.8 = ((bf16[8,1152,128]{2,1,0:T(8,128)(2,1)}), bf16[8,1152,128]{2,1,0:T(8,128)(2,1)S(1)}, u32[]{:S(2)}, u32[]{:S(2)}) async-start(bf16[8,1152,128]{2,1,0:T(8,128)(2,1)} %bitcast.281), calls=%async_computation.8 | async-start | bytes 4718592 | tf_op jit(solution)/shard_map/all_to_all | solution.py:62
  450.9 2.2 copy-start.8
  454.2 15.8 %collective-permute-start.2 = (bf16[128,32,128]{2,0,1:T(8,128)(2,1)S(1)}, bf16[128,32,128]{2,0,1:T(8,128)(2,1)S(1)}, u32[]{:S(2)}, u32[]{:S(2)}) collective-permute-start(bf16[128,32,128]{2,0,1:T(8,128)(2,1)S(1)} %fusion.37), channel_id=1, source_target_pairs={{0,120},{8,0},{16,8},{24,16},{32,24},{40,32},{48,40},{56,48},{64,5... | collective-permute-start | bytes 3145736 | tf_op jit(solution)/shard_map/ppermute | solution.py:9

commit v3 on v2

--- a/solution.py
+++ b/solution.py
@@ -63,18 +63,23 @@
         return moved.reshape(groups, capacity, pieces, lanes)
 
     plans = [route_plan(step) for step in range(rounds)]
-    forwards = []
-    for step in range(rounds):
-        rows = saved_inputs[step, 0].reshape(rows_dev, pieces, lanes)
-        input_part = exchange(collect(plans[step][0], rows))
-        forwards.append(forward_part(input_part, gate_proj, up_proj))
+    input_buffers = [
+        collect(plans[step][0], saved_inputs[step, 0].reshape(rows_dev, pieces, lanes))
+        for step in range(rounds)
+    ]
+    pre_gate, pre_up = forward_part(exchange(input_buffers[0]), gate_proj, up_proj)
 
     present_block = grad_in[0].reshape(rows_dev, pieces, lanes)
     for step in range(rounds):
         dispatch, weights_hi, weights_lo = plans[step]
         grad_part = exchange(collect(dispatch, present_block))
-        pre_gate, pre_up = forwards[step]
+        if step + 1 < rounds:
+            grad_part, next_buffer = lax.optimization_barrier((grad_part, input_buffers[step + 1]))
+            next_part = exchange(next_buffer)
         result = backward_part(grad_part, pre_gate, pre_up, gate_proj, up_proj, down_proj)
+        if step + 1 < rounds:
+            result, next_part = lax.optimization_barrier((result, next_part))
+            pre_gate, pre_up = forward_part(next_part, gate_proj, up_proj)
         arrived = exchange(result)
         combined = jnp.einsum("tec,ecjl->tjl", weights_hi, arrived, preferred_element_type=jnp.float32)
         combined = combined + jnp.einsum("tec,ecjl->tjl", weights_lo, arrived, preferred_element_type=jnp.float32)

time: 479 us -> 461 us (0.962)
  the two profiles are of different devices: /device:TPU:1 before, /device:TPU:91 now
where the time goes in v3:
time: 461 us; the launch traced here: 453 us
  waiting for transfers between devices  225 us (49%)
  matrix products  126 us (27%)
  starting transfers between devices  54 us (12%)
  local copies, waits for them, and re-layouts  44.8 us (10%)
    all_to_all x9, waiting for transfers between devices, exchange(): lax.all_to_all(flat, 'expert', split_axis=0, concat_axis=0, tiled=True)  175 us
    all_to_all x9, starting transfers between devices, exchange(): lax.all_to_all(flat, 'expert', split_axis=0, concat_axis=0, tiled=True)  49.7 us
    ppermute x3, waiting for transfers between devices, shifted(): lax.ppermute(x, axis, [(i, (i + by) % devices) for i in range(devices)])  49.4 us
    dot_general x3, matrix products, backward_part(): jnp.einsum('sch,jlh->scjl', grad_gate, gate_proj, preferred_element_type=...  41.1 us
    dot_general x3, matrix products, backward_part(): jnp.einsum('sch,jlh->scjl', grad_up, up_proj, preferred_element_type=jnp....  25.3 us
    dot_general x3, matrix products, backward_part(): jnp.einsum('scjl,hjl->sch', grad_part, down_proj, preferred_element_type=...  23.2 us
    dot_general x3, matrix products, forward_part(): jnp.einsum('scjl,jlh->sch', input_part, gate_proj, preferred_element_type...  19.4 us
    unnamed x55, local copies, waits for them, and re-layouts  13.4 us
  transfers between devices with their start and end apart: 12, of which 12 were waited for; matrix products, arithmetic and copies ran while one was open for 22% of the time, Pallas kernels for 0%

profile of v3, /device:TPU:91, one launch (start us, length us, event | category | flops | bytes accessed | tf_op | source)
XLA Modules:
  0.0 453.1 jit_solution(12608066030253003424)
XLA Ops:
  5.7 5.2 %all-to-all-start = ((bf16[8,1152,128]{2,1,0:T(8,128)(2,1)}), bf16[8,1152,128]{2,1,0:T(8,128)(2,1)}, u32[]{:S(2)}, u32[]{:S(2)}) async-start(bf16[8,1152,128]{2,1,0:T(8,128)(2,1)} %bitcast.7), calls=%async_computation | async-start | bytes 4718592 | tf_op jit(solution)/shard_map/all_to_all | solution.py:62
  17.8 24.3 %all-to-all-done = bf16[8,1152,128]{2,1,0:T(8,128)(2,1)} async-done(((bf16[8,1152,128]{2,1,0:T(8,128)(2,1)}), bf16[8,1152,128]{2,1,0:T(8,128)(2,1)}, u32[]{:S(2)}, u32[]{:S(2)}) %all-to-all-start) | async-done | bytes 2359328 | tf_op jit(solution)/shard_map/all_to_all | solution.py:62
  50.0 4.9 %copy.132 = bf16[96,8,32,128]{3,2,1,0:T(8,128)(2,1)S(1)} copy(bf16[96,8,32,128]{3,1,2,0:T(8,128)(2,1)} %bitcast.282) | data formatting | bytes 12582912
  58.2 6.7 %fusion.66 = f32[8,36,768]{2,1,0:T(8,128)} fusion(bf16[768,32,128]{2,1,0:T(8,128)(2,1)S(1)} %bitcast.283, bf16[8,36,32,128]{3,2,1,0:T(8,128)(2,1)} %bitcast.8), kind=kOutput, calls=%fused_computation.60 | convolution fusion | flops 1811939328 | bytes 9535488 | tf_op jit(solution)/shard_map/scjl,hjl->sch/dot_general | solution.py:19
  64.9 9.8 %all-to-all-done.1 = bf16[8,1152,128]{2,1,0:T(8,128)(2,1)S(1)} async-done(((bf16[8,1152,128]{2,1,0:T(8,128)(2,1)}), bf16[8,1152,128]{2,1,0:T(8,128)(2,1)S(1)}, u32[]{:S(2)}, u32[]{:S(2)}) %all-to-all-start.1) | async-done | bytes 2359328 | tf_op jit(solution)/shard_map/all_to_all | solution.py:62
  76.2 5.8 %all-to-all-start.2 = ((bf16[8,1152,128]{2,1,0:T(8,128)(2,1)}), bf16[8,1152,128]{2,1,0:T(8,128)(2,1)S(1)}, u32[]{:S(2)}, u32[]{:S(2)}) async-start(bf16[8,1152,128]{2,1,0:T(8,128)(2,1)} %bitcast.277), calls=%async_computation.2 | async-start | bytes 4718592 | tf_op jit(solution)/shard_map/all_to_all | solution.py:62
  82.0 7.1 %fusion.51 = f32[8,36,768]{2,1,0:T(8,128)} fusion(bf16[32,128,768,1]{2,1,0,3:T(8,128)(2,1)} %bitcast.258, bf16[8,36,32,128]{3,2,1,0:T(8,128)(2,1)} %bitcast.272), kind=kOutput, calls=%fused_computation.55 | convolution fusion | flops 1811939328 | bytes 9535488 | tf_op jit(solution)/shard_map/scjl,jlh->sch/dot_general | solution.py:13
  89.2 14.0 %fusion.129 = f32[8,36,32,128]{3,1,2,0:T(8,128)} fusion(bf16[32,128,768,1]{2,1,0,3:T(8,128)(2,1)} %bitcast.259, f32[8,36,768]{2,1,0:T(8,128)} %fusion.66, bf16[32,128,768,1]{2,1,0,3:T(8,128)(2,1)} %bitcast.252, bf16[8,36,32,128]{3,2,1,0:T(8,128)(2,1)} %bitcast.273, f32[8,36,768]{2,1,0:T(8,128)} %fusion.51), kind=kOutput, calls=%fused_computation.88 | convolution fusion | flops 3626090496 | bytes 21430272 | tf_op jit(solution)/shard_map/sch,jlh->scjl/dot_general | solution.py:24
  103.2 8.7 %add_convert_fusion.2 = bf16[8,36,32,128]{3,1,2,0:T(8,128)(2,1)} fusion(f32[8,36,32,128]{3,1,2,0:T(8,128)} %fusion.129, bf16[32,128,768,1]{2,1,0,3:T(8,128)(2,1)} %bitcast.253, f32[8,36,768]{2,1,0:T(8,128)} %fusion.66, f32[8,36,768]{2,1,0:T(8,128)} %fusion.51), kind=kOutput, calls=%fused_computation.8 | convolution fusion | flops 1815625728 | bytes 15138816 | tf_op jit(solution)/shard_map/sch,jlh->scjl/dot_general | solution.py:25
  118.2 5.0 %all-to-all-start.3 = ((bf16[8,1152,128]{2,1,0:T(8,128)(2,1)}), bf16[8,1152,128]{2,1,0:T(8,128)(2,1)S(1)}, u32[]{:S(2)}, u32[]{:S(2)}) async-start(bf16[8,1152,128]{2,1,0:T(8,128)(2,1)} %bitcast.278), calls=%async_computation.3 | async-start | bytes 4718592 | tf_op jit(solution)/shard_map/all_to_all | solution.py:62
  126.5 24.6 %all-to-all-done.3 = bf16[8,1152,128]{2,1,0:T(8,128)(2,1)S(1)} async-done(((bf16[8,1152,128]{2,1,0:T(8,128)(2,1)}), bf16[8,1152,128]{2,1,0:T(8,128)(2,1)S(1)}, u32[]{:S(2)}, u32[]{:S(2)}) %all-to-all-start.3) | async-done | bytes 2359328 | tf_op jit(solution)/shard_map/all_to_all | solution.py:62
  155.7 15.8 %collective-permute-done = bf16[128,32,128]{2,0,1:T(8,128)(2,1)S(1)} collective-permute-done((bf16[128,32,128]{2,0,1:T(8,128)(2,1)S(1)}, bf16[128,32,128]{2,0,1:T(8,128)(2,1)S(1)}, u32[]{:S(2)}, u32[]{:S(2)}) %collective-permute-start) | collective-permute-done | bytes 1048608 | tf_op jit(solution)/shard_map/ppermute | solution.py:9
  174.2 6.4 %all-to-all-start.4 = ((bf16[8,1152,128]{2,1,0:T(8,128)(2,1)}), bf16[8,1152,128]{2,1,0:T(8,128)(2,1)}, u32[]{:S(2)}, u32[]{:S(2)}) async-start(bf16[8,1152,128]{2,1,0:T(8,128)(2,1)} %bitcast.46), calls=%async_computation.4 | async-start | bytes 4718592 | tf_op jit(solution)/shard_map/all_to_all | solution.py:62
  184.8 5.1 %fusion.57 = f32[8,36,768]{2,1,0:T(8,128)S(1)} fusion(bf16[32,128,768,1]{2,1,0,3:T(8,128)(2,1)} %bitcast.260, bf16[8,36,32,128]{3,2,1,0:T(8,128)(2,1)S(1)} %bitcast.270), kind=kOutput, calls=%fused_computation.57 | convolution fusion | flops 1811939328 | bytes 9535488 | tf_op jit(solution)/shard_map/scjl,jlh->sch/dot_general | solution.py:13
  190.0 15.6 %all-to-all-done.4 = bf16[8,1152,128]{2,1,0:T(8,128)(2,1)} async-done(((bf16[8,1152,128]{2,1,0:T(8,128)(2,1)}), bf16[8,1152,128]{2,1,0:T(8,128)(2,1)}, u32[]{:S(2)}, u32[]{:S(2)}) %all-to-all-start.4) | async-done | bytes 2359328 | tf_op jit(solution)/shard_map/all_to_all | solution.py:62
  205.6 8.7 %fusion.71 = f32[8,36,768]{2,1,0:T(8,128)} fusion(bf16[768,32,128]{2,1,0:T(8,128)(2,1)} %bitcast.284, bf16[8,36,32,128]{3,2,1,0:T(8,128)(2,1)} %bitcast.47), kind=kOutput, calls=%fused_computation.61 | convolution fusion | flops 1811939328 | bytes 9535488 | tf_op jit(solution)/shard_map/scjl,hjl->sch/dot_general | solution.py:19
  216.2 6.7 %all-to-all-start.5 = ((bf16[8,1152,128]{2,1,0:T(8,128)(2,1)}), bf16[8,1152,128]{2,1,0:T(8,128)(2,1)}, u32[]{:S(2)}, u32[]{:S(2)}) async-start(bf16[8,1152,128]{2,1,0:T(8,128)(2,1)} %bitcast.279), calls=%async_computation.5 | async-start | bytes 4718592 | tf_op jit(solution)/shard_map/all_to_all | solution.py:62
  222.9 13.0 %fusion.126 = f32[8,36,32,128]{3,1,2,0:T(8,128)} fusion(bf16[32,128,768,1]{2,1,0,3:T(8,128)(2,1)} %bitcast.261, f32[8,36,768]{2,1,0:T(8,128)} %fusion.71, bf16[32,128,768,1]{2,1,0,3:T(8,128)(2,1)} %bitcast.254, bf16[8,36,32,128]{3,2,1,0:T(8,128)(2,1)S(1)} %bitcast.271, f32[8,36,768]{2,1,0:T(8,128)S(1)} %fusion.57), kind=kOutput, calls=%fused_computation.87 | convolution fusion | flops 3626090496 | bytes 21430272 | tf_op jit(solution)/shard_map/sch,jlh->scjl/dot_general | solution.py:24
  236.0 8.4 %add_convert_fusion.1 = bf16[8,36,32,128]{3,1,2,0:T(8,128)(2,1)} fusion(f32[8,36,32,128]{3,1,2,0:T(8,128)} %fusion.126, bf16[32,128,768,1]{2,1,0,3:T(8,128)(2,1)} %bitcast.255, f32[8,36,768]{2,1,0:T(8,128)} %fusion.71, f32[8,36,768]{2,1,0:T(8,128)S(1)} %fusion.57), kind=kOutput, calls=%fused_computation.7 | convolution fusion | flops 1815625728 | bytes 15138816 | tf_op jit(solution)/shard_map/sch,jlh->scjl/dot_general | solution.py:25
  244.3 13.1 %all-to-all-done.5 = bf16[8,1152,128]{2,1,0:T(8,128)(2,1)} async-done(((bf16[8,1152,128]{2,1,0:T(8,128)(2,1)}), bf16[8,1152,128]{2,1,0:T(8,128)(2,1)}, u32[]{:S(2)}, u32[]{:S(2)}) %all-to-all-start.5) | async-done | bytes 2359328 | tf_op jit(solution)/shard_map/all_to_all | solution.py:62
  261.2 5.0 %all-to-all-start.6 = ((bf16[8,1152,128]{2,1,0:T(8,128)(2,1)}), bf16[8,1152,128]{2,1,0:T(8,128)(2,1)S(1)}, u32[]{:S(2)}, u32[]{:S(2)}) async-start(bf16[8,1152,128]{2,1,0:T(8,128)(2,1)} %bitcast.281), calls=%async_computation.6 | async-start | bytes 4718592 | tf_op jit(solution)/shard_map/all_to_all | solution.py:62
  266.9 28.2 %all-to-all-done.6 = bf16[8,1152,128]{2,1,0:T(8,128)(2,1)S(1)} async-done(((bf16[8,1152,128]{2,1,0:T(8,128)(2,1)}), bf16[8,1152,128]{2,1,0:T(8,128)(2,1)S(1)}, u32[]{:S(2)}, u32[]{:S(2)}) %all-to-all-start.6) | async-done | bytes 2359328 | tf_op jit(solution)/shard_map/all_to_all | solution.py:62
  300.9 17.5 %collective-permute-done.1 = bf16[128,32,128]{2,0,1:T(8,128)(2,1)S(1)} collective-permute-done((bf16[128,32,128]{2,0,1:T(8,128)(2,1)S(1)}, bf16[128,32,128]{2,0,1:T(8,128)(2,1)S(1)}, u32[]{:S(2)}, u32[]{:S(2)}) %collective-permute-start.1) | collective-permute-done | bytes 1048608 | tf_op jit(solution)/shard_map/ppermute | solution.py:9
  321.2 5.7 %all-to-all-start.7 = ((bf16[8,1152,128]{2,1,0:T(8,128)(2,1)}), bf16[8,1152,128]{2,1,0:T(8,128)(2,1)S(1)}, u32[]{:S(2)}, u32[]{:S(2)}) async-start(bf16[8,1152,128]{2,1,0:T(8,128)(2,1)} %bitcast.77), calls=%async_computation.7 | async-start | bytes 4718592 | tf_op jit(solution)/shard_map/all_to_all | solution.py:62
  326.9 7.1 %fusion.63 = f32[8,36,768]{2,1,0:T(8,128)} fusion(bf16[32,128,768,1]{2,1,0,3:T(8,128)(2,1)} %bitcast.262, bf16[8,36,32,128]{3,2,1,0:T(8,128)(2,1)} %bitcast.66), kind=kOutput, calls=%fused_computation.59 | convolution fusion | flops 1811939328 | bytes 9535488 | tf_op jit(solution)/shard_map/scjl,jlh->sch/dot_general | solution.py:13
  334.0 23.9 %all-to-all-done.7 = bf16[8,1152,128]{2,1,0:T(8,128)(2,1)S(1)} async-done(((bf16[8,1152,128]{2,1,0:T(8,128)(2,1)}), bf16[8,1152,128]{2,1,0:T(8,128)(2,1)S(1)}, u32[]{:S(2)}, u32[]{:S(2)}) %all-to-all-start.7) | async-done | bytes 2359328 | tf_op jit(solution)/shard_map/all_to_all | solution.py:62
  357.8 7.8 %fusion.76 = f32[8,36,768]{2,1,0:T(8,128)} fusion(bf16[768,32,128]{2,1,0:T(8,128)(2,1)} %bitcast.285, bf16[8,36,32,128]{3,2,1,0:T(8,128)(2,1)S(1)} %bitcast.290), kind=kOutput, calls=%fused_computation.62 | convolution fusion | flops 1811939328 | bytes 9535488 | tf_op jit(solution)/shard_map/scjl,hjl->sch/dot_general | solution.py:19
  365.7 14.1 %fusion.123 = f32[8,36,32,128]{3,1,2,0:T(8,128)} fusion(bf16[32,128,768,1]{2,1,0,3:T(8,128)(2,1)} %bitcast.263, f32[8,36,768]{2,1,0:T(8,128)} %fusion.76, bf16[32,128,768,1]{2,1,0,3:T(8,128)(2,1)} %bitcast.256, bf16[8,36,32,128]{3,2,1,0:T(8,128)(2,1)} %bitcast.66, f32[8,36,768]{2,1,0:T(8,128)} %fusion.63), kind=kOutput, calls=%fused_computation.86 | convolution fusion | flops 3626090496 | bytes 21430272 | tf_op jit(solution)/shard_map/sch,jlh->scjl/dot_general | solution.py:24
  379.8 8.2 %add_convert_fusion = bf16[8,36,32,128]{3,1,2,0:T(8,128)(2,1)S(1)} fusion(f32[8,36,32,128]{3,1,2,0:T(8,128)} %fusion.123, bf16[32,128,768,1]{2,1,0,3:T(8,128)(2,1)} %bitcast.257, f32[8,36,768]{2,1,0:T(8,128)S(1)} %copy-done.13, f32[8,36,768]{2,1,0:T(8,128)S(1)} %copy-done.12), kind=kOutput, calls=%fused_computation.6 | convolution fusion | flops 1815625728 | bytes 15138816 | tf_op jit(solution)/shard_map/sch,jlh->scjl/dot_general | solution.py:25
  389.9 5.0 %all-to-all-start.8 = ((bf16[8,1152,128]{2,1,0:T(8,128)(2,1)}), bf16[8,1152,128]{2,1,0:T(8,128)(2,1)S(1)}, u32[]{:S(2)}, u32[]{:S(2)}) async-start(bf16[8,1152,128]{2,1,0:T(8,128)(2,1)} %bitcast.280), calls=%async_computation.8 | async-start | bytes 4718592 | tf_op jit(solution)/shard_map/all_to_all | solution.py:62
  396.3 34.3 %all-to-all-done.8 = bf16[8,1152,128]{2,1,0:T(8,128)(2,1)S(1)} async-done(((bf16[8,1152,128]{2,1,0:T(8,128)(2,1)}), bf16[8,1152,128]{2,1,0:T(8,128)(2,1)S(1)}, u32[]{:S(2)}, u32[]{:S(2)}) %all-to-all-start.8) | async-done | bytes 2359328 | tf_op jit(solution)/shard_map/all_to_all | solution.py:62
  434.5 16.2 %collective-permute-done.2 = bf16[128,32,128]{2,0,1:T(8,128)(2,1)S(1)} collective-permute-done((bf16[128,32,128]{2,0,1:T(8,128)(2,1)S(1)}, bf16[128,32,128]{2,0,1:T(8,128)(2,1)S(1)}, u32[]{:S(2)}, u32[]{:S(2)}) %collective-permute-start.2) | collective-permute-done | bytes 1048608 | tf_op jit(solution)/shard_map/ppermute | solution.py:9
  (97 shorter events, 70.4 us)
Async XLA Ops:
  0.8 46.2 %copy-start.19 = (s32[128,2]{0,1:T(2,128)}, s32[128,2]{0,1:T(2,128)S(1)}, u32[]{:S(2)}) copy-start(s32[128,2]{0,1:T(2,128)S(1)} %get-tuple-element.24) | copy-start | bytes 3076
  0.8 46.2 %copy-start.20 = (s32[128,2]{0,1:T(2,128)}, s32[128,2]{0,1:T(2,128)S(1)}, u32[]{:S(2)}) copy-start(s32[128,2]{0,1:T(2,128)S(1)} %get-tuple-element.26) | copy-start | bytes 3076
  5.7 36.4 %all-to-all-start = ((bf16[8,1152,128]{2,1,0:T(8,128)(2,1)}), bf16[8,1152,128]{2,1,0:T(8,128)(2,1)}, u32[]{:S(2)}, u32[]{:S(2)}) async-start(bf16[8,1152,128]{2,1,0:T(8,128)(2,1)} %bitcast.7), calls=%async_computation | async-start | bytes 4718592 | tf_op jit(solution)/shard_map/all_to_all | solution.py:62
  42.1 32.7 %all-to-all-start.1 = ((bf16[8,1152,128]{2,1,0:T(8,128)(2,1)}), bf16[8,1152,128]{2,1,0:T(8,128)(2,1)S(1)}, u32[]{:S(2)}, u32[]{:S(2)}) async-start(bf16[8,1152,128]{2,1,0:T(8,128)(2,1)} %bitcast.276), calls=%async_computation.1 | async-start | bytes 4718592 | tf_op jit(solution)/shard_map/all_to_all | solution.py:62
  47.6 7.2 %copy-start.14 = (pred[8,36,128,1]{2,1,0,3:T(8,128)(4,1)}, pred[8,36,128,1]{2,1,0,3:T(8,128)(4,1)S(1)}, u32[]{:S(2)}) copy-start(pred[8,36,128,1]{2,1,0,3:T(8,128)(4,1)S(1)} %reshape.171) | copy-start | bytes 110596
  50.0 4.9 %copy-start.5 = (bf16[1,1,128,4096]{2,3,1,0:T(8,128)(2,1)S(1)}, bf16[1,1,128,4096]{2,3,1,0:T(8,128)(2,1)}, u32[]{:S(2)}) copy-start(bf16[1,1,128,4096]{2,3,1,0:T(8,128)(2,1)} %copy.129) | copy-start | bytes 3145732
  54.9 3.3 copy-start.4
  76.2 37.4 %all-to-all-start.2 = ((bf16[8,1152,128]{2,1,0:T(8,128)(2,1)}), bf16[8,1152,128]{2,1,0:T(8,128)(2,1)S(1)}, u32[]{:S(2)}, u32[]{:S(2)}) async-start(bf16[8,1152,128]{2,1,0:T(8,128)(2,1)} %bitcast.277), calls=%async_computation.2 | async-start | bytes 4718592 | tf_op jit(solution)/shard_map/all_to_all | solution.py:62
  113.6 4.6 %copy-start = (bf16[8,1152,128]{2,1,0:T(8,128)(2,1)}, bf16[8,1152,128]{2,1,0:T(8,128)(2,1)S(1)}, u32[]{:S(2)}) copy-start(bf16[8,1152,128]{2,1,0:T(8,128)(2,1)S(1)} %all-to-all-done.2) | copy-start | bytes 7077892
  118.2 5.0 %copy-start.24 = (f32[3,1,128,2]{2,3,1,0:T(2,128)S(1)}, f32[3,1,128,2]{2,3,1,0:T(2,128)}, u32[]{:S(2)}) copy-start(f32[3,1,128,2]{2,3,1,0:T(2,128)} %param.12) | copy-start | bytes 9220
  118.2 32.8 %all-to-all-start.3 = ((bf16[8,1152,128]{2,1,0:T(8,128)(2,1)}), bf16[8,1152,128]{2,1,0:T(8,128)(2,1)S(1)}, u32[]{:S(2)}, u32[]{:S(2)}) async-start(bf16[8,1152,128]{2,1,0:T(8,128)(2,1)} %bitcast.278), calls=%async_computation.3 | async-start | bytes 4718592 | tf_op jit(solution)/shard_map/all_to_all | solution.py:62
  126.5 26.7 %copy-start.8 = (bf16[128,32,128]{2,0,1:T(8,128)(2,1)S(1)}, bf16[128,32,128]{2,0,1:T(8,128)(2,1)}, u32[]{:S(2)}) copy-start(bf16[128,32,128]{2,0,1:T(8,128)(2,1)} %copy.60) | copy-start | bytes 3145732
  153.2 18.3 %copy-start.15 = (pred[8,36,128,1]{2,1,0,3:T(8,128)(4,1)S(1)}, pred[8,36,128,1]{2,1,0,3:T(8,128)(4,1)}, u32[]{:S(2)}) copy-start(pred[8,36,128,1]{2,1,0,3:T(8,128)(4,1)} %copy-done.14) | copy-start | bytes 110596
  154.4 17.1 %collective-permute-start = (bf16[128,32,128]{2,0,1:T(8,128)(2,1)S(1)}, bf16[128,32,128]{2,0,1:T(8,128)(2,1)S(1)}, u32[]{:S(2)}, u32[]{:S(2)}) collective-permute-start(bf16[128,32,128]{2,0,1:T(8,128)(2,1)S(1)} %fusion.41), channel_id=1, source_target_pairs={{0,120},{8,0},{16,8},{24,16},{32,24},{40,32},{48,40},{56,48},{64,5... | collective-permute-start | bytes 3145736 | tf_op jit(solution)/shard_map/ppermute | solution.py:9
  171.5 2.7 copy-start.6
  174.2 6.4 %copy-start.18 = (pred[128,288]{0,1:T(8,128)(4,1)S(1)}, pred[128,288]{0,1:T(8,128)(4,1)}, u32[]{:S(2)}) copy-start(pred[128,288]{0,1:T(8,128)(4,1)} %get-tuple-element.30) | copy-start | bytes 110596
  174.2 31.4 %all-to-all-start.4 = ((bf16[8,1152,128]{2,1,0:T(8,128)(2,1)}), bf16[8,1152,128]{2,1,0:T(8,128)(2,1)}, u32[]{:S(2)}, u32[]{:S(2)}) async-start(bf16[8,1152,128]{2,1,0:T(8,128)(2,1)} %bitcast.46), calls=%async_computation.4 | async-start | bytes 4718592 | tf_op jit(solution)/shard_map/all_to_all | solution.py:62
  180.7 4.2 copy-start.16
  180.7 4.2 copy-start.1
  205.6 8.7 %copy-start.3 = (bf16[8,36,32,128]{3,1,2,0:T(8,128)(2,1)S(1)}, bf16[8,36,32,128]{3,1,2,0:T(8,128)(2,1)}, u32[]{:S(2)}) copy-start(bf16[8,36,32,128]{3,1,2,0:T(8,128)(2,1)} %convolution_convert_fusion.1) | copy-start | bytes 7077892
  216.2 41.3 %all-to-all-start.5 = ((bf16[8,1152,128]{2,1,0:T(8,128)(2,1)}), bf16[8,1152,128]{2,1,0:T(8,128)(2,1)}, u32[]{:S(2)}, u32[]{:S(2)}) async-start(bf16[8,1152,128]{2,1,0:T(8,128)(2,1)} %bitcast.279), calls=%async_computation.5 | async-start | bytes 4718592 | tf_op jit(solution)/shard_map/all_to_all | solution.py:62
  261.2 5.0 %copy-start.21 = (s32[128,2]{0,1:T(2,128)S(1)}, s32[128,2]{0,1:T(2,128)}, u32[]{:S(2)}) copy-start(s32[128,2]{0,1:T(2,128)} %copy-done.20) | copy-start | bytes 3076
  261.2 5.0 %copy-start.23 = (f32[128,2]{0,1:T(2,128)S(1)}, f32[128,2]{0,1:T(2,128)}, u32[]{:S(2)}) copy-start(f32[128,2]{0,1:T(2,128)} %get-tuple-element.29) | copy-start | bytes 3076
  261.2 33.9 %all-to-all-start.6 = ((bf16[8,1152,128]{2,1,0:T(8,128)(2,1)}), bf16[8,1152,128]{2,1,0:T(8,128)(2,1)S(1)}, u32[]{:S(2)}, u32[]{:S(2)}) async-start(bf16[8,1152,128]{2,1,0:T(8,128)(2,1)} %bitcast.281), calls=%async_computation.6 | async-start | bytes 4718592 | tf_op jit(solution)/shard_map/all_to_all | solution.py:62
  266.2 31.0 %copy-start.7 = (bf16[128,32,128]{2,0,1:T(8,128)(2,1)S(1)}, bf16[128,32,128]{2,0,1:T(8,128)(2,1)}, u32[]{:S(2)}) copy-start(bf16[128,32,128]{2,0,1:T(8,128)(2,1)} %copy-done.6) | copy-start | bytes 3145732
  297.3 21.1 %copy-start.17 = (pred[8,36,128,1]{2,1,0,3:T(8,128)(4,1)S(1)}, pred[8,36,128,1]{2,1,0,3:T(8,128)(4,1)}, u32[]{:S(2)}) copy-start(pred[8,36,128,1]{2,1,0,3:T(8,128)(4,1)} %copy-done.16) | copy-start | bytes 110596
  298.4 19.9 %collective-permute-start.1 = (bf16[128,32,128]{2,0,1:T(8,128)(2,1)S(1)}, bf16[128,32,128]{2,0,1:T(8,128)(2,1)S(1)}, u32[]{:S(2)}, u32[]{:S(2)}) collective-permute-start(bf16[128,32,128]{2,0,1:T(8,128)(2,1)S(1)} %fusion.39), channel_id=1, source_target_pairs={{0,120},{8,0},{16,8},{24,16},{32,24},{40,32},{48,40},{56,48},{64,5... | collective-permute-start | bytes 3145736 | tf_op jit(solution)/shard_map/ppermute | solution.py:9
  321.2 36.7 %all-to-all-start.7 = ((bf16[8,1152,128]{2,1,0:T(8,128)(2,1)}), bf16[8,1152,128]{2,1,0:T(8,128)(2,1)S(1)}, u32[]{:S(2)}, u32[]{:S(2)}) async-start(bf16[8,1152,128]{2,1,0:T(8,128)(2,1)} %bitcast.77), calls=%async_computation.7 | async-start | bytes 4718592 | tf_op jit(solution)/shard_map/all_to_all | solution.py:62
  365.7 14.1 %copy-start.12 = (f32[8,36,768]{2,1,0:T(8,128)S(1)}, f32[8,36,768]{2,1,0:T(8,128)}, u32[]{:S(2)}) copy-start(f32[8,36,768]{2,1,0:T(8,128)} %fusion.63) | copy-start | bytes 2654212
  365.7 14.1 %copy-start.13 = (f32[8,36,768]{2,1,0:T(8,128)S(1)}, f32[8,36,768]{2,1,0:T(8,128)}, u32[]{:S(2)}) copy-start(f32[8,36,768]{2,1,0:T(8,128)} %fusion.76) | copy-start | bytes 2654212
  389.9 40.7 %all-to-all-start.8 = ((bf16[8,1152,128]{2,1,0:T(8,128)(2,1)}), bf16[8,1152,128]{2,1,0:T(8,128)(2,1)S(1)}, u32[]{:S(2)}, u32[]{:S(2)}) async-start(bf16[8,1152,128]{2,1,0:T(8,128)(2,1)} %bitcast.280), calls=%async_computation.8 | async-start | bytes 4718592 | tf_op jit(solution)/shard_map/all_to_all | solution.py:62
  433.9 16.7 %collective-permute-start.2 = (bf16[128,32,128]{2,0,1:T(8,128)(2,1)S(1)}, bf16[128,32,128]{2,0,1:T(8,128)(2,1)S(1)}, u32[]{:S(2)}, u32[]{:S(2)}) collective-permute-start(bf16[128,32,128]{2,0,1:T(8,128)(2,1)S(1)} %fusion.37), channel_id=1, source_target_pairs={{0,120},{8,0},{16,8},{24,16},{32,24},{40,32},{48,40},{56,48},{64,5... | collective-permute-start | bytes 3145736 | tf_op jit(solution)/shard_map/ppermute | solution.py:9
  (5 other events, 8.5 us)
